TPU v7x, 256 devices: a whole 4x4x8 slice. The times are simulated.
256 devices in a mesh: grp: 8 (over z_lo, core), ep: 32 (over z_hi, y, x).
Axes of the slice: x: 4, y: 4, z: 8 (z_hi: 2, z_lo: 4; z = z_hi * 4 + z_lo), core: 2. Of those that a mesh axis runs over, the one named last changes fastest.
Arguments:
- tokens_in: bfloat16 [32768, 2048], P(('grp', 'ep')), may hold values from -6 to 6
- grad_out: bfloat16 [32768, 2048], P(('grp', 'ep')), may hold values from -6 to 6
- replica_of: int32 [32768, 2], P(('grp', 'ep')), may hold values from 0 to 255, all different within a row; in each aligned block of 128 rows (0 to 127, 128 to 255, ...) at most 2 rows name the same one
- gate_weights: bfloat16 [32768, 2], P(('grp', 'ep')), may hold values from 0.099609375 to 1
- placement: int32 [8, 32], replicated, may hold values from 0 to 1, as said below
- w_in_rep: bfloat16 [8, 32, 2048, 1024], P('grp', 'ep'), as said below
- w_down_rep: bfloat16 [8, 32, 2048, 512], P('grp', 'ep'), as said below
Outputs:
- d_tokens: bfloat16 [32768, 2048], P(('grp', 'ep'))
- d_gates: bfloat16 [32768, 2], P(('grp', 'ep'))
- grad_in: bfloat16 [64, 2048, 1024], P('ep', 'grp')
- grad_down: bfloat16 [64, 2048, 512], P('ep', 'grp')
Inputs may be any that keep to these rules, and one draw needn't show every extreme that they name: `replica_of`: A row names a replica device by its index in the order grp then ep. The 2 rows of a token name different devices. At most 2 of the rows of one device name the same replica device, and some device sends exactly 2 rows to one replica. placement[g, e] selects expert e * 2 + placement[g, e]; in every column e each of the 2 values occurs at least once, so every expert has at least one copy. w_in_rep[g, e] and w_in_rep[g2, e] are equal wherever placement[g, e] equals placement[g2, e]. w_down_rep[g, e] and w_down_rep[g2, e] are equal wherever placement[g, e] equals placement[g2, e].
All inputs are finite; a program needn't handle non-finite values.
Results may differ from a plain program's by a relative error of at most 0.01.
Values may be sent and summed in bfloat16 or wider, within the bound.
No kernel may reach another device: no remote copies, remote signals or barrier semaphores. Data moves between devices by JAX's collectives and lax.ppermute only.
A program may use at most 128 MiB of HBM per device.

v0:
```python
import jax
import jax.numpy as jnp
from jax import lax
from jax.sharding import PartitionSpec as P

KPC = 2


def expert_backward(rows_x, rows_dy, rows_gate, w_in, w_down):
    hidden = w_down.shape[1]
    both = jnp.dot(rows_x, w_in, preferred_element_type=jnp.float32)
    gate_pre = both[:, :hidden]
    up_part = both[:, hidden:]
    sigmoid_gate = jax.nn.sigmoid(gate_pre)
    silu_gate = gate_pre * sigmoid_gate
    activation = (silu_gate * up_part).astype(jnp.bfloat16)
    out_rows = lax.dot_general(
        activation, w_down, (((1,), (1,)), ((), ())), preferred_element_type=jnp.float32
    )
    gate_grad = jnp.sum(rows_dy.astype(jnp.float32) * out_rows, axis=1).astype(jnp.bfloat16)
    out_grad = (rows_gate.astype(jnp.float32)[:, None] * rows_dy.astype(jnp.float32)).astype(
        jnp.bfloat16
    )
    act_grad = jnp.dot(out_grad, w_down, preferred_element_type=jnp.float32)
    gate_grad_pre = act_grad * up_part * sigmoid_gate * (1.0 + gate_pre * (1.0 - sigmoid_gate))
    up_grad = act_grad * silu_gate
    both_grad = jnp.concatenate([gate_grad_pre, up_grad], axis=1).astype(jnp.bfloat16)
    row_grad = lax.dot_general(
        both_grad, w_in, (((1,), (1,)), ((), ())), preferred_element_type=jnp.float32
    ).astype(jnp.bfloat16)
    part_in = lax.dot_general(
        rows_x, both_grad, (((0,), (0,)), ((), ())), preferred_element_type=jnp.float32
    )
    part_down = lax.dot_general(
        out_grad, activation, (((0,), (0,)), ((), ())), preferred_element_type=jnp.float32
    )
    return (row_grad, gate_grad, part_in, part_down)


def shards(tokens_in, grad_out, replica_of, gate_weights, placement, w_in_rep, w_down_rep):
    tok_count, model_width = tokens_in.shape
    top_count = replica_of.shape[1]
    group_count = lax.axis_size("grp")
    lane_count = lax.axis_size("ep")
    device_count = group_count * lane_count
    capacity = max(2, 2 * tok_count * top_count // device_count)
    w_in = w_in_rep[0, 0]
    w_down = w_down_rep[0, 0]
    dest_rows = replica_of.reshape(-1)
    row_count = tok_count * top_count
    row_ids = jnp.arange(row_count, dtype=jnp.int32)
    earlier = (dest_rows[:, None] == dest_rows[None, :]) & (row_ids[None, :] < row_ids[:, None])
    rank_in = jnp.sum(earlier.astype(jnp.int32), axis=1)
    send_slot = dest_rows * capacity + rank_in
    slot_table = jnp.full((device_count * capacity,), -1, jnp.int32).at[send_slot].set(row_ids)
    is_live = slot_table >= 0
    safe_ids = jnp.maximum(slot_table, 0)
    token_ids = safe_ids // top_count
    send_x = jnp.where(is_live[:, None], tokens_in[token_ids], jnp.zeros((), tokens_in.dtype))
    send_dy = jnp.where(is_live[:, None], grad_out[token_ids], jnp.zeros((), grad_out.dtype))
    send_gate = jnp.where(
        is_live, gate_weights.reshape(-1)[safe_ids], jnp.zeros((), gate_weights.dtype)
    )
    block_shape = (group_count, lane_count, capacity, model_width)
    outgoing = (
        send_x.reshape(block_shape),
        send_dy.reshape(block_shape),
        send_gate.reshape(group_count, lane_count, capacity),
    )
    arrived = (
        lax.all_to_all(
            lax.all_to_all(outgoing[0], "ep", split_axis=1, concat_axis=1, tiled=True),
            "grp",
            split_axis=0,
            concat_axis=0,
            tiled=True,
        ),
        lax.all_to_all(
            lax.all_to_all(outgoing[1], "ep", split_axis=1, concat_axis=1, tiled=True),
            "grp",
            split_axis=0,
            concat_axis=0,
            tiled=True,
        ),
        lax.all_to_all(
            lax.all_to_all(outgoing[2], "ep", split_axis=1, concat_axis=1, tiled=True),
            "grp",
            split_axis=0,
            concat_axis=0,
            tiled=True,
        ),
    )
    rows_x = arrived[0].reshape(device_count * capacity, model_width)
    rows_dy = arrived[1].reshape(device_count * capacity, model_width)
    rows_gate = arrived[2].reshape(device_count * capacity)
    row_grad, gate_grad, part_in, part_down = expert_backward(
        rows_x, rows_dy, rows_gate, w_in, w_down
    )
    returning = (
        row_grad.reshape(block_shape),
        gate_grad.reshape(group_count, lane_count, capacity),
    )
    came_back = (
        lax.all_to_all(
            lax.all_to_all(returning[0], "grp", split_axis=0, concat_axis=0, tiled=True),
            "ep",
            split_axis=1,
            concat_axis=1,
            tiled=True,
        ),
        lax.all_to_all(
            lax.all_to_all(returning[1], "grp", split_axis=0, concat_axis=0, tiled=True),
            "ep",
            split_axis=1,
            concat_axis=1,
            tiled=True,
        ),
    )
    grads_rows = came_back[0].reshape(device_count * capacity, model_width)[send_slot]
    d_tokens = jnp.sum(
        grads_rows.reshape(tok_count, top_count, model_width).astype(jnp.float32), axis=1
    ).astype(jnp.bfloat16)
    d_gates = came_back[1].reshape(-1)[send_slot].reshape(tok_count, top_count)
    group_index = lax.axis_index("grp")
    column_index = lax.axis_index("ep")
    my_slot = placement[group_index, column_index]
    slot_mask = (jnp.arange(KPC, dtype=jnp.int32) == my_slot).astype(jnp.float32)
    stack_in = slot_mask[:, None, None] * part_in[None]
    stack_down = slot_mask[:, None, None] * part_down[None]
    summed_in, summed_down = (
        lax.psum_scatter(
            stack_in.astype(jnp.bfloat16), "grp", scatter_dimension=1, tiled=True
        ).astype(jnp.float32),
        lax.psum_scatter(
            stack_down.astype(jnp.bfloat16), "grp", scatter_dimension=1, tiled=True
        ).astype(jnp.float32),
    )
    return (d_tokens, d_gates, summed_in.astype(jnp.bfloat16), summed_down.astype(jnp.bfloat16))


def solution(mesh):
    placed = (
        P(("grp", "ep"), None),
        P(("grp", "ep"), None),
        P(("grp", "ep"), None),
        P(("grp", "ep"), None),
        P(),
        P("grp", "ep", None, None),
        P("grp", "ep", None, None),
    )
    return jax.shard_map(
        shards,
        mesh=mesh,
        in_specs=placed,
        out_specs=(
            P(("grp", "ep"), None),
            P(("grp", "ep"), None),
            P("ep", "grp", None),
            P("ep", "grp", None),
        ),
        check_vma=False,
    )
```

profile of v0, /device:TPU:1, one launch (start us, length us, event | category | flops | bytes accessed | tf_op | source)
XLA Modules:
  0.0 533.8 jit_solution(1596756059104067243)
XLA Ops:
  7.2 0.8 broadcast_multiply_fusion
  8.0 0.8 copy.100
  8.8 0.8 copy.101
  10.2 0.2 convert_reduce_fusion
  10.4 1.4 scatter_custom_fusion
  11.8 3.4 gather_fusion
  15.2 0.2 reshape.105
  15.3 0.9 copy.102
  16.2 14.5 %all-to-all-start = ((bf16[8,32,2]{0,2,1:T(2,128)(2,1)}), bf16[8,32,2]{0,2,1:T(2,128)(2,1)S(1)}, u32[]{:S(2)}, u32[]{:S(2)}) async-start(bf16[8,32,2]{0,2,1:T(2,128)(2,1)} %copy.102), calls=%async_computation | async-start | bytes 32768 | tf_op jit(solution)/shard_map/all_to_all | solution.py:86
  30.7 0.2 broadcast_in_dim.47
  30.9 3.3 gather_fusion.2
  34.2 4.5 gather.23
  38.7 3.3 gather_fusion.1
  42.0 4.4 gather.21
  46.4 0.7 copy.103
  47.1 4.2 all-to-all-start.1
  51.3 7.1 %broadcast_select_fusion = (bf16[8,32,2,2048]{3,2,0,1:T(2,128)(2,1)}, bf16[8,32,2,2048]{3,2,0,1:T(2,128)(2,1)}) fusion(pred[8,32,2]{2,0,1:T(8,128)(4,1)S(1)} %copy.106, bf16[8,32,2,2048]{3,2,1,0:T(2,128)(2,1)} %gather.23, bf16[8,32,2,2048]{3,2,1,0:T(2,128)(2,1)} %gather.21), kind=kLoop, calls=%fused_computation.15 | loop fusion | flops 2097152 | bytes 8389120 | tf_op jit(solution)/shard_map/jit(_where)/select_n | solution.py:59
  58.4 42.9 %all_to_all.50 = bf16[8,32,2,2048]{3,2,0,1:T(2,128)(2,1)} all-to-all(bf16[8,32,2,2048]{3,2,0,1:T(2,128)(2,1)} %get-tuple-element.34), channel_id=1, replica_groups=mesh['grp'=8,'ep'=32] {'ep'}, dimensions={1} | all-to-all | bytes 4194304 | tf_op jit(solution)/shard_map/all_to_all | solution.py:79
  101.2 5.8 %all-to-all-start.4 = ((bf16[8,32,2,2048]{3,2,0,1:T(2,128)(2,1)}), bf16[8,32,2,2048]{3,2,0,1:T(2,128)(2,1)}, u32[]{:S(2)}, u32[]{:S(2)}) async-start(bf16[8,32,2,2048]{3,2,0,1:T(2,128)(2,1)} %get-tuple-element.33), calls=%async_computation.4 | async-start | bytes 4194304 | tf_op jit(solution)/shard_map/all_to_all | solution.py:72
  107.0 4.7 copy.108
  111.7 24.7 %all-to-all-done.4 = bf16[8,32,2,2048]{3,2,0,1:T(2,128)(2,1)} async-done(((bf16[8,32,2,2048]{3,2,0,1:T(2,128)(2,1)}), bf16[8,32,2,2048]{3,2,0,1:T(2,128)(2,1)}, u32[]{:S(2)}, u32[]{:S(2)}) %all-to-all-start.4) | async-done | bytes 2097184 | tf_op jit(solution)/shard_map/all_to_all | solution.py:72
  136.3 45.6 %all-to-all-start.3 = ((bf16[8,32,2,2048]{3,2,1,0:T(2,128)(2,1)}), bf16[8,32,2,2048]{3,2,1,0:T(2,128)(2,1)}, u32[]{:S(2)}, u32[]{:S(2)}) async-start(bf16[8,32,2,2048]{3,2,1,0:T(2,128)(2,1)} %copy.108), calls=%async_computation.3 | async-start | bytes 4194304 | tf_op jit(solution)/shard_map/all_to_all | solution.py:78
  181.9 4.6 copy.110
  186.6 43.5 %all-to-all-done.3 = bf16[8,32,2,2048]{3,2,1,0:T(2,128)(2,1)} async-done(((bf16[8,32,2,2048]{3,2,1,0:T(2,128)(2,1)}), bf16[8,32,2,2048]{3,2,1,0:T(2,128)(2,1)}, u32[]{:S(2)}, u32[]{:S(2)}) %all-to-all-start.3) | async-done | bytes 2097184 | tf_op jit(solution)/shard_map/all_to_all | solution.py:78
  230.1 5.2 all-to-all-start.5
  235.3 0.5 reduce-scatter.5.cloned.1.call-start
  235.7 1.3 dynamic_slice.3
  237.0 0.6 compare_convert_fusion
  238.0 4.7 multiply_convert_fusion.3
  242.6 4.2 convert_element_type.71
  246.8 36.7 %all-to-all-done.5 = bf16[8,32,2,2048]{3,2,1,0:T(2,128)(2,1)} async-done(((bf16[8,32,2,2048]{3,2,1,0:T(2,128)(2,1)}), bf16[8,32,2,2048]{3,2,1,0:T(2,128)(2,1)}, u32[]{:S(2)}, u32[]{:S(2)}) %all-to-all-start.5) | async-done | bytes 2097184 | tf_op jit(solution)/shard_map/all_to_all | solution.py:71
  283.5 4.1 reshape.106
  287.6 5.3 %fusion.2 = f32[512,1024]{0,1:T(8,128)S(1)} fusion(bf16[512,2048]{1,0:T(8,128)(2,1)} %reshape.106, bf16[1,1,2048,1024]{3,2,1,0:T(8,128)(2,1)} %param.12), kind=kOutput, calls=%fused_computation.10 | convolution fusion | flops 2147483648 | bytes 8388608 | tf_op jit(solution)/shard_map/dot_general | solution.py:11
  293.0 2.5 multiply_convert_fusion.7
  295.5 4.4 reshape.112
  299.9 3.6 fusion.7
  303.6 2.8 multiply_convert_fusion.1
  306.4 0.2 reduce-scatter.3.cloned.1.call-start
  306.6 7.3 %fusion.13 = f32[2048,1024]{1,0:T(8,128)} fusion(bf16[512,2048]{1,0:T(8,128)(2,1)} %reshape.106, bf16[512,512]{0,1:T(8,128)(2,1)} %get-tuple-element.31, bf16[512,512]{0,1:T(8,128)(2,1)S(1)} %get-tuple-element.30), kind=kOutput, calls=%fused_computation.29 | convolution fusion | flops 2149580800 | bytes 11534336 | tf_op jit(solution)/shard_map/dot_general | solution.py:31
  314.0 8.7 %multiply_convert_fusion = bf16[2,2048,1024]{2,1,0:T(8,128)(2,1)} fusion(f32[2048,1024]{1,0:T(8,128)} %fusion.13, f32[2]{0:T(128)S(1)} %compare_convert_fusion), kind=kLoop, calls=%fused_computation.6 | loop fusion | flops 8388608 | bytes 16777224 | tf_op jit(solution)/shard_map/convert_element_type | solution.py:132
  322.6 3.6 multiply_reduce_fusion
  326.3 0.2 convert_element_type.77
  326.5 0.7 copy.115
  327.2 4.2 all-to-all-start.8
  331.3 6.1 %fusion.4 = bf16[512,2048]{1,0:T(8,128)(2,1)} fusion(bf16[1,1,2048,1024]{3,2,1,0:T(8,128)(2,1)} %param.12, bf16[512,512]{0,1:T(8,128)(2,1)} %get-tuple-element.31, bf16[512,512]{0,1:T(8,128)(2,1)S(1)} %get-tuple-element.30), kind=kOutput, calls=%fused_computation.17 | convolution fusion | flops 2150629376 | bytes 7340032 | tf_op jit(solution)/shard_map/dot_general | solution.py:28
  337.5 4.5 reshape.107
  342.0 5.1 all-to-all-start.6
  347.1 0.7 copy.116
  347.8 59.6 %all-to-all-done.6 = bf16[8,32,2,2048]{3,2,1,0:T(2,128)(2,1)} async-done(((bf16[8,32,2,2048]{3,2,1,0:T(2,128)(2,1)}), bf16[8,32,2,2048]{3,2,1,0:T(2,128)(2,1)}, u32[]{:S(2)}, u32[]{:S(2)}) %all-to-all-start.6) | async-done | bytes 2097184 | tf_op jit(solution)/shard_map/all_to_all | solution.py:105
  407.4 10.3 %all-to-all-start.9 = ((bf16[8,32,2]{0,2,1:T(2,128)(2,1)}), bf16[8,32,2]{0,2,1:T(2,128)(2,1)S(1)}, u32[]{:S(2)}, u32[]{:S(2)}) async-start(bf16[8,32,2]{0,2,1:T(2,128)(2,1)} %copy.116), calls=%async_computation.9 | async-start | bytes 32768 | tf_op jit(solution)/shard_map/all_to_all | solution.py:111
  417.7 5.2 copy.113
  422.9 5.9 %all-to-all-done.9 = bf16[8,32,2]{0,2,1:T(2,128)(2,1)S(1)} async-done(((bf16[8,32,2]{0,2,1:T(2,128)(2,1)}), bf16[8,32,2]{0,2,1:T(2,128)(2,1)S(1)}, u32[]{:S(2)}, u32[]{:S(2)}) %all-to-all-start.9) | async-done | bytes 1056 | tf_op jit(solution)/shard_map/all_to_all | solution.py:111
  428.8 6.2 %all-to-all-start.7 = ((bf16[8,32,2,2048]{3,2,0,1:T(2,128)(2,1)}), bf16[8,32,2,2048]{3,2,0,1:T(2,128)(2,1)}, u32[]{:S(2)}, u32[]{:S(2)}) async-start(bf16[8,32,2,2048]{3,2,0,1:T(2,128)(2,1)} %copy.113), calls=%async_computation.7 | async-start | bytes 4194304 | tf_op jit(solution)/shard_map/all_to_all | solution.py:104
  435.0 0.3 copy.117
  435.3 0.1 reshape.110
  435.4 1.9 gather_fusion.4
  437.4 0.2 reshape.111
  437.5 0.6 copy.119
  438.1 69.4 %all-to-all-done.7 = bf16[8,32,2,2048]{3,2,0,1:T(2,128)(2,1)} async-done(((bf16[8,32,2,2048]{3,2,0,1:T(2,128)(2,1)}), bf16[8,32,2,2048]{3,2,0,1:T(2,128)(2,1)}, u32[]{:S(2)}, u32[]{:S(2)}) %all-to-all-start.7) | async-done | bytes 2097184 | tf_op jit(solution)/shard_map/all_to_all | solution.py:104
  507.5 4.7 copy.114
  512.2 4.2 reshape.108
  516.3 4.2 gather_fusion.3
  520.6 1.5 reshape.109
  522.1 4.6 reduce_sum.34
  (29 shorter events, 0.9 us)
Async XLA Ops:
  7.2 285.8 %copy-start = (bf16[1,1,2048,512]{3,2,1,0:T(8,128)(2,1)S(1)}, bf16[1,1,2048,512]{3,2,1,0:T(8,128)(2,1)}, u32[]{:S(2)}) copy-start(bf16[1,1,2048,512]{3,2,1,0:T(8,128)(2,1)} %param.13) | copy-start | bytes 6291460
  7.2 23.8 %copy-start.1 = (bf16[128,2048]{1,0:T(8,128)(2,1)S(1)}, bf16[128,2048]{1,0:T(8,128)(2,1)}, u32[]{:S(2)}) copy-start(bf16[128,2048]{1,0:T(8,128)(2,1)} %param.7) | copy-start | bytes 1572868
  16.2 30.2 %all-to-all-start = ((bf16[8,32,2]{0,2,1:T(2,128)(2,1)}), bf16[8,32,2]{0,2,1:T(2,128)(2,1)S(1)}, u32[]{:S(2)}, u32[]{:S(2)}) async-start(bf16[8,32,2]{0,2,1:T(2,128)(2,1)} %copy.102), calls=%async_computation | async-start | bytes 32768 | tf_op jit(solution)/shard_map/all_to_all | solution.py:86
  34.2 4.5 copy-start.2
  47.1 11.2 %all-to-all-start.1 = ((bf16[8,32,2]{1,2,0:T(2,128)(2,1)}), bf16[8,32,2]{1,2,0:T(2,128)(2,1)S(1)}, u32[]{:S(2)}, u32[]{:S(2)}) async-start(bf16[8,32,2]{1,2,0:T(2,128)(2,1)} %copy.103), calls=%async_computation.1 | async-start | bytes 8192 | tf_op jit(solution)/shard_map/all_to_all | solution.py:85
  101.2 35.1 %all-to-all-start.4 = ((bf16[8,32,2,2048]{3,2,0,1:T(2,128)(2,1)}), bf16[8,32,2,2048]{3,2,0,1:T(2,128)(2,1)}, u32[]{:S(2)}, u32[]{:S(2)}) async-start(bf16[8,32,2,2048]{3,2,0,1:T(2,128)(2,1)} %get-tuple-element.33), calls=%async_computation.4 | async-start | bytes 4194304 | tf_op jit(solution)/shard_map/all_to_all | solution.py:72
  136.3 93.8 %all-to-all-start.3 = ((bf16[8,32,2,2048]{3,2,1,0:T(2,128)(2,1)}), bf16[8,32,2,2048]{3,2,1,0:T(2,128)(2,1)}, u32[]{:S(2)}, u32[]{:S(2)}) async-start(bf16[8,32,2,2048]{3,2,1,0:T(2,128)(2,1)} %copy.108), calls=%async_computation.3 | async-start | bytes 4194304 | tf_op jit(solution)/shard_map/all_to_all | solution.py:78
  230.1 53.4 %all-to-all-start.5 = ((bf16[8,32,2,2048]{3,2,1,0:T(2,128)(2,1)}), bf16[8,32,2,2048]{3,2,1,0:T(2,128)(2,1)}, u32[]{:S(2)}, u32[]{:S(2)}) async-start(bf16[8,32,2,2048]{3,2,1,0:T(2,128)(2,1)} %copy.110), calls=%async_computation.5 | async-start | bytes 4194304 | tf_op jit(solution)/shard_map/all_to_all | solution.py:71
  235.3 291.4 %reduce-scatter.5.cloned.1.call-start = ((), (), s32[]{:S(2)}) async-start(), calls=%async_computation.13 | async-start | bytes 4718592 | tf_op jit(solution)/shard_map/reduce_scatter | solution.py:134
  287.6 5.4 %copy-start.3 = (bf16[512,2048]{1,0:T(8,128)(2,1)S(1)}, bf16[512,2048]{1,0:T(8,128)(2,1)}, u32[]{:S(2)}) copy-start(bf16[512,2048]{1,0:T(8,128)(2,1)} %convert_element_type.71) | copy-start | bytes 6291460
  306.4 220.3 %reduce-scatter.3.cloned.1.call-start = ((), (), s32[]{:S(2)}) async-start(), calls=%async_computation.12 | async-start | bytes 9437184 | tf_op jit(solution)/shard_map/reduce_scatter | solution.py:131
  327.2 14.8 %all-to-all-start.8 = ((bf16[8,32,2]{1,2,0:T(2,128)(2,1)}), bf16[8,32,2]{1,2,0:T(2,128)(2,1)S(1)}, u32[]{:S(2)}, u32[]{:S(2)}) async-start(bf16[8,32,2]{1,2,0:T(2,128)(2,1)} %copy.115), calls=%async_computation.8 | async-start | bytes 8192 | tf_op jit(solution)/shard_map/all_to_all | solution.py:112
  342.0 65.4 %all-to-all-start.6 = ((bf16[8,32,2,2048]{3,2,1,0:T(2,128)(2,1)}), bf16[8,32,2,2048]{3,2,1,0:T(2,128)(2,1)}, u32[]{:S(2)}, u32[]{:S(2)}) async-start(bf16[8,32,2,2048]{3,2,1,0:T(2,128)(2,1)} %reshape.107), calls=%async_computation.6 | async-start | bytes 4194304 | tf_op jit(solution)/shard_map/all_to_all | solution.py:105
  407.4 21.4 %all-to-all-start.9 = ((bf16[8,32,2]{0,2,1:T(2,128)(2,1)}), bf16[8,32,2]{0,2,1:T(2,128)(2,1)S(1)}, u32[]{:S(2)}, u32[]{:S(2)}) async-start(bf16[8,32,2]{0,2,1:T(2,128)(2,1)} %copy.116), calls=%async_computation.9 | async-start | bytes 32768 | tf_op jit(solution)/shard_map/all_to_all | solution.py:111
  428.8 78.7 %all-to-all-start.7 = ((bf16[8,32,2,2048]{3,2,0,1:T(2,128)(2,1)}), bf16[8,32,2,2048]{3,2,0,1:T(2,128)(2,1)}, u32[]{:S(2)}, u32[]{:S(2)}) async-start(bf16[8,32,2,2048]{3,2,0,1:T(2,128)(2,1)} %copy.113), calls=%async_computation.7 | async-start | bytes 4194304 | tf_op jit(solution)/shard_map/all_to_all | solution.py:104
Sparse Core Ops, SparseCore 0:
  306.5 53.7 reduce-scatter.4
  363.4 162.2 reduce-scatter.2
where the time goes:
time: 544 us; the launch traced here: 534 us
  waiting for transfers between devices  240 us (44%)
  starting transfers between devices  102 us (19%)
  local copies, waits for them, and re-layouts  76.9 us (14%)
  blocking collectives  42.9 us (8%)
  other arithmetic  29.5 us (5%)
  matrix products  28.6 us (5%)
  between operations  14.5 us (3%)
    all_to_all x1, waiting for transfers between devices, shards(): lax.all_to_all(lax.all_to_all(returning[0], 'grp', split_axis=0, concat_a...  69.4 us
    all_to_all x1, waiting for transfers between devices, shards(): lax.all_to_all(returning[0], 'grp', split_axis=0, concat_axis=0, tiled=True)  59.6 us
    all_to_all x1, starting transfers between devices, shards(): lax.all_to_all(lax.all_to_all(outgoing[1], 'ep', split_axis=1, concat_axi...  45.6 us
    all_to_all x1, waiting for transfers between devices, shards(): lax.all_to_all(lax.all_to_all(outgoing[1], 'ep', split_axis=1, concat_axi...  43.5 us
    all_to_all x1, blocking collectives, shards(): lax.all_to_all(outgoing[1], 'ep', split_axis=1, concat_axis=1, tiled=True)  42.9 us
    all_to_all x1, waiting for transfers between devices, shards(): lax.all_to_all(lax.all_to_all(outgoing[0], 'ep', split_axis=1, concat_axi...  36.7 us
    all_to_all x1, waiting for transfers between devices, shards(): lax.all_to_all(outgoing[0], 'ep', split_axis=1, concat_axis=1, tiled=True)  24.7 us
    all_to_all x1, starting transfers between devices, shards(): lax.all_to_all(outgoing[2], 'ep', split_axis=1, concat_axis=1, tiled=True)  14.5 us
  transfers between devices with their start and end apart: 11, of which 6 were waited for; matrix products, arithmetic and copies ran while one was open for 19% of the time, Pallas kernels for 0%

commit v1 on v0

--- a/solution.py
+++ b/solution.py
@@ -61,66 +61,32 @@
     send_gate = jnp.where(
         is_live, gate_weights.reshape(-1)[safe_ids], jnp.zeros((), gate_weights.dtype)
     )
-    block_shape = (group_count, lane_count, capacity, model_width)
-    outgoing = (
-        send_x.reshape(block_shape),
-        send_dy.reshape(block_shape),
-        send_gate.reshape(group_count, lane_count, capacity),
+    lane_pad = 128
+    gate_cols = jnp.zeros((device_count * capacity, lane_pad), send_x.dtype).at[:, 0].set(send_gate)
+    outgoing = jnp.concatenate([send_x, send_dy, gate_cols], axis=1).reshape(
+        device_count, capacity, 2 * model_width + lane_pad
     )
-    arrived = (
-        lax.all_to_all(
-            lax.all_to_all(outgoing[0], "ep", split_axis=1, concat_axis=1, tiled=True),
-            "grp",
-            split_axis=0,
-            concat_axis=0,
-            tiled=True,
-        ),
-        lax.all_to_all(
-            lax.all_to_all(outgoing[1], "ep", split_axis=1, concat_axis=1, tiled=True),
-            "grp",
-            split_axis=0,
-            concat_axis=0,
-            tiled=True,
-        ),
-        lax.all_to_all(
-            lax.all_to_all(outgoing[2], "ep", split_axis=1, concat_axis=1, tiled=True),
-            "grp",
-            split_axis=0,
-            concat_axis=0,
-            tiled=True,
-        ),
+    arrived = lax.all_to_all(outgoing, ("grp", "ep"), 0, 0, tiled=True).reshape(
+        device_count * capacity, 2 * model_width + lane_pad
     )
-    rows_x = arrived[0].reshape(device_count * capacity, model_width)
-    rows_dy = arrived[1].reshape(device_count * capacity, model_width)
-    rows_gate = arrived[2].reshape(device_count * capacity)
+    rows_x = arrived[:, :model_width]
+    rows_dy = arrived[:, model_width : 2 * model_width]
+    rows_gate = arrived[:, 2 * model_width]
     row_grad, gate_grad, part_in, part_down = expert_backward(
         rows_x, rows_dy, rows_gate, w_in, w_down
     )
-    returning = (
-        row_grad.reshape(block_shape),
-        gate_grad.reshape(group_count, lane_count, capacity),
+    back_cols = jnp.zeros((device_count * capacity, lane_pad), row_grad.dtype).at[:, 0].set(gate_grad)
+    returning = jnp.concatenate([row_grad, back_cols], axis=1).reshape(
+        device_count, capacity, model_width + lane_pad
     )
-    came_back = (
-        lax.all_to_all(
-            lax.all_to_all(returning[0], "grp", split_axis=0, concat_axis=0, tiled=True),
-            "ep",
-            split_axis=1,
-            concat_axis=1,
-            tiled=True,
-        ),
-        lax.all_to_all(
-            lax.all_to_all(returning[1], "grp", split_axis=0, concat_axis=0, tiled=True),
-            "ep",
-            split_axis=1,
-            concat_axis=1,
-            tiled=True,
-        ),
-    )
-    grads_rows = came_back[0].reshape(device_count * capacity, model_width)[send_slot]
+    came_back = lax.all_to_all(returning, ("grp", "ep"), 0, 0, tiled=True).reshape(
+        device_count * capacity, model_width + lane_pad
+    )[send_slot]
+    grads_rows = came_back[:, :model_width]
     d_tokens = jnp.sum(
         grads_rows.reshape(tok_count, top_count, model_width).astype(jnp.float32), axis=1
     ).astype(jnp.bfloat16)
-    d_gates = came_back[1].reshape(-1)[send_slot].reshape(tok_count, top_count)
+    d_gates = came_back[:, model_width].reshape(tok_count, top_count)
     group_index = lax.axis_index("grp")
     column_index = lax.axis_index("ep")
     my_slot = placement[group_index, column_index]

time: 544 us -> 358 us (0.66); the launches traced: 534 us -> 356 us
  starting transfers between devices: 102 us -> 25.3 us
  blocking collectives: 42.9 us -> 0 us
  local copies, waits for them, and re-layouts: 76.9 us -> 47.1 us
  waiting for transfers between devices: 240 us -> 220 us
  matrix products: 28.6 us -> 22.2 us
    all_to_all x9 -> x2, waiting for transfers between devices: 240 us -> 162 us  [the longest x1 96.8 us: shards(): lax.all_to_all(outgoing, ('grp', 'ep'), 0, 0, tiled=True)]
    all_to_all x9 -> x2, starting transfers between devices: 101 us -> 24.8 us  [the longest x1 16.5 us: shards(): lax.all_to_all(outgoing, ('grp', 'ep'), 0, 0, tiled=True)]
    reduce_scatter x1, waiting for transfers between devices: 0.01 us -> 58 us  [shards(): lax.psum_scatter(stack_in.astype(jnp.bfloat16), 'grp', scatter_dimension=...]
    all_to_all x1 -> x0, blocking collectives: 42.9 us -> none  [shards(): lax.all_to_all(outgoing[1], 'ep', split_axis=1, concat_axis=1, tiled=True)]
    all_to_all x7 -> x0, local copies, waits for them, and re-layouts: 20.9 us -> none  [the longest x1 5.2 us: shards(): lax.all_to_all(returning[0], 'grp', split_axis=0, concat_axis=0, tiled=True)]
    convert_element_type x6 -> x0, local copies, waits for them, and re-layouts: 9.78 us -> none  [the longest x1 4.44 us: expert_backward(): rows_dy.astype(jnp.float32)]
    reshape x7 -> x4, local copies, waits for them, and re-layouts: 14.1 us -> 23 us  [the longest x1 7.35 us: shards(): jnp.concatenate([send_x, send_dy, gate_cols], axis=1)]
  transfers between devices with their start and end apart: 11 -> 4, of which waited for: 6 -> 3; matrix products, arithmetic and copies ran while one was open for 19% -> 13% of each run, Pallas kernels for 0% -> 0%
where the time goes in v1:
time: 358 us; the launch traced here: 356 us
  waiting for transfers between devices  220 us (61%)
  local copies, waits for them, and re-layouts  47.1 us (13%)
  other arithmetic  26.9 us (8%)
  starting transfers between devices  25.3 us (7%)
  matrix products  22.2 us (6%)
  between operations  14.3 us (4%)
    all_to_all x1, waiting for transfers between devices, shards(): lax.all_to_all(outgoing, ('grp', 'ep'), 0, 0, tiled=True)  96.8 us
    all_to_all x1, waiting for transfers between devices, shards(): lax.all_to_all(returning, ('grp', 'ep'), 0, 0, tiled=True)  65.2 us
    reduce_scatter x1, waiting for transfers between devices, shards(): lax.psum_scatter(stack_in.astype(jnp.bfloat16), 'grp', scatter_dimension=...  58 us
    all_to_all x1, starting transfers between devices, shards(): lax.all_to_all(outgoing, ('grp', 'ep'), 0, 0, tiled=True)  16.5 us
    convert_element_type x1, other arithmetic, shards(): stack_in.astype(jnp.bfloat16)  8.65 us
    all_to_all x1, starting transfers between devices, shards(): lax.all_to_all(returning, ('grp', 'ep'), 0, 0, tiled=True)  8.29 us
    reshape x1, local copies, waits for them, and re-layouts, shards(): jnp.concatenate([send_x, send_dy, gate_cols], axis=1)  7.35 us
    dot_general x1, matrix products, expert_backward(): lax.dot_general(rows_x, both_grad, (((0,), (0,)), ((), ())), preferred_el...  7.29 us
  transfers between devices with their start and end apart: 4, of which 3 were waited for; matrix products, arithmetic and copies ran while one was open for 13% of the time, Pallas kernels for 0%

profile of v1, /device:TPU:1, one launch (start us, length us, event | category | flops | bytes accessed | tf_op | source)
XLA Modules:
  0.0 356.0 jit_solution(16266509711628112445)
XLA Ops:
  7.2 0.0 copy-start
  7.2 0.0 copy-start.1
  7.2 0.6 compare_reduce_fusion
  7.8 0.7 broadcast_multiply_fusion
  8.5 0.8 copy.23
  9.3 0.8 copy.24
  10.1 0.1 reshape.129
  10.3 0.1 copy.22
  10.4 0.1 mul.81
  10.5 0.1 eq.25
  10.7 0.2 convert_reduce_fusion.1
  10.9 1.4 scatter_custom_fusion
  12.3 3.4 gather_fusion.2
  15.7 0.7 select_select_fusion
  16.3 0.1 reshape.181
  16.5 0.0 copy-done.1
  16.5 0.0 copy-start.2
  16.5 3.3 gather_fusion.1
  19.8 0.0 copy-done.2
  19.8 3.3 gather_fusion
  23.1 2.6 broadcast_select_fusion.1
  25.7 2.2 fusion.2
  27.9 7.3 %reshape.131 = bf16[256,2,4224]{2,1,0:T(2,128)(2,1)} reshape(bf16[512,4224]{1,0:T(8,128)(2,1)} %fusion.2) | data formatting | bytes 8650752 | tf_op jit(solution)/shard_map/reshape | solution.py:66
  35.2 16.5 %all-to-all-start = ((bf16[256,2,4224]{2,1,0:T(2,128)(2,1)}), bf16[256,2,4224]{2,1,0:T(2,128)(2,1)}, u32[]{:S(2)}, u32[]{:S(2)}) async-start(bf16[256,2,4224]{2,1,0:T(2,128)(2,1)} %reshape.131), calls=%async_computation | async-start | bytes 8650752 | tf_op jit(solution)/shard_map/all_to_all | solution.py:69
  51.7 0.2 reduce-scatter.5.cloned.1.call-start
  52.0 1.3 dynamic_slice.3
  53.3 0.6 compare_convert_fusion
  53.9 96.8 %all-to-all-done = bf16[256,2,4224]{2,1,0:T(2,128)(2,1)} async-done(((bf16[256,2,4224]{2,1,0:T(2,128)(2,1)}), bf16[256,2,4224]{2,1,0:T(2,128)(2,1)}, u32[]{:S(2)}, u32[]{:S(2)}) %all-to-all-start) | async-done | bytes 4325408 | tf_op jit(solution)/shard_map/all_to_all | solution.py:69
  150.7 7.3 %reshape.132 = bf16[512,4224]{1,0:T(8,128)(2,1)} reshape(bf16[256,2,4224]{2,1,0:T(2,128)(2,1)} %all-to-all-done) | data formatting | bytes 8650752 | tf_op jit(solution)/shard_map/reshape | solution.py:69
  158.0 1.0 convert_reduce_fusion
  159.0 0.0 copy-start.3
  159.0 5.3 %fusion.7 = f32[512,1024]{0,1:T(8,128)S(1)} fusion(bf16[1,1,2048,1024]{3,2,1,0:T(8,128)(2,1)} %param.16, bf16[512,4224]{1,0:T(8,128)(2,1)} %reshape.132), kind=kOutput, calls=%fused_computation.18 | convolution fusion | flops 2147483648 | bytes 8388608 | tf_op jit(solution)/shard_map/dot_general | solution.py:11
  164.4 0.0 copy-done
  164.4 0.0 copy-done.3
  164.4 2.6 multiply_convert_fusion.4
  167.0 1.5 fusion.20
  168.4 2.8 multiply_convert_fusion.1
  171.3 0.0 reduce-scatter.5.cloned.1.call-update
  171.3 0.3 reduce-scatter.3.cloned.1.call-start
  171.6 7.3 %fusion.16 = f32[2048,1024]{1,0:T(8,128)} fusion(bf16[512,4224]{1,0:T(8,128)(2,1)} %reshape.132, bf16[512,512]{0,1:T(8,128)(2,1)} %get-tuple-element.43, bf16[512,512]{0,1:T(8,128)(2,1)S(1)} %get-tuple-element.42), kind=kOutput, calls=%fused_computation.27 | convolution fusion | flops 2149580800 | bytes 11534336 | tf_op jit(solution)/shard_map/dot_general | solution.py:31
  178.9 8.6 %multiply_convert_fusion = bf16[2,2048,1024]{2,1,0:T(8,128)(2,1)} fusion(f32[2048,1024]{1,0:T(8,128)} %fusion.16, f32[2]{0:T(128)S(1)} %compare_convert_fusion), kind=kLoop, calls=%fused_computation.5 | loop fusion | flops 8388608 | bytes 16777224 | tf_op jit(solution)/shard_map/convert_element_type | solution.py:98
  187.5 0.0 reduce-scatter.3.cloned.1.call-update
  187.5 0.0 copy-start.4
  187.5 0.0 copy-start.5
  187.6 3.1 fusion.4
  190.7 0.7 convert_select_fusion
  191.4 0.1 reshape.182
  191.5 0.0 copy-done.4
  191.5 0.0 copy-done.5
  191.5 2.4 fusion.9
  193.9 1.6 fusion.12
  195.5 4.2 %reshape.134 = bf16[256,2,2176]{2,1,0:T(2,128)(2,1)} reshape(bf16[512,2176]{1,0:T(8,128)(2,1)} %fusion.12) | data formatting | bytes 4456448 | tf_op jit(solution)/shard_map/reshape | solution.py:79
  199.7 8.3 %all-to-all-start.1 = ((bf16[256,2,2176]{2,1,0:T(2,128)(2,1)}), bf16[256,2,2176]{2,1,0:T(2,128)(2,1)}, u32[]{:S(2)}, u32[]{:S(2)}) async-start(bf16[256,2,2176]{2,1,0:T(2,128)(2,1)} %reshape.134), calls=%async_computation.1 | async-start | bytes 4456448 | tf_op jit(solution)/shard_map/all_to_all | solution.py:82
  208.0 65.2 %all-to-all-done.1 = bf16[256,2,2176]{2,1,0:T(2,128)(2,1)} async-done(((bf16[256,2,2176]{2,1,0:T(2,128)(2,1)}), bf16[256,2,2176]{2,1,0:T(2,128)(2,1)}, u32[]{:S(2)}, u32[]{:S(2)}) %all-to-all-start.1) | async-done | bytes 2228256 | tf_op jit(solution)/shard_map/all_to_all | solution.py:82
  273.3 4.2 %reshape.135 = bf16[512,2176]{1,0:T(8,128)(2,1)} reshape(bf16[256,2,2176]{2,1,0:T(2,128)(2,1)} %all-to-all-done.1) | data formatting | bytes 4456448 | tf_op jit(solution)/shard_map/reshape | solution.py:82
  277.5 4.4 %gather_fusion.3 = bf16[256,2176]{1,0:T(8,128)(2,1)S(1)} fusion(bf16[512,2176]{1,0:T(8,128)(2,1)} %reshape.135, s32[1024]{0:T(1024)S(1)} %pad_clamp_fusion), kind=kCustom, calls=%fused_computation.3 | custom fusion | bytes 2229248 | tf_op jit(solution)/shard_map/gather | solution.py:82
  281.9 1.2 slice.69
  283.1 2.5 reshape.136
  285.7 0.1 slice_reduce_fusion
  285.8 0.2 reshape_squeeze.3
  285.9 0.6 copy.29
  286.5 4.6 %reduce_sum.35 = bf16[128,2048]{1,0:T(8,128)(2,1)} reduce(bf16[128,2,2048]{2,1,0:T(2,128)(2,1)} %reshape.136, bf16[]{:T(256)} %constant.86.clone.1), dimensions={1}, to_apply=%region_4.5 | reduce | flops 262144 | bytes 1572866 | tf_op jit(solution)/shard_map/reduce_sum | solution.py:86
  291.1 0.0 reduce-scatter.5.cloned.1.call-done
  291.1 58.0 %reduce-scatter.3.cloned.1.call-done = bf16[2,256,1024]{2,1,0:T(8,128)(2,1)} async-done(((bf16[2,2048,1024]{2,1,0:T(8,128)(2,1)}), bf16[2,256,1024]{2,1,0:T(8,128)(2,1)}) %reduce-scatter.3.cloned.1.call-update) | async-done | bytes 1048592 | tf_op jit(solution)/shard_map/reduce_scatter | solution.py:97
  (5 shorter events, 0.0 us)
Async XLA Ops:
  7.2 157.2 %copy-start = (bf16[1,1,2048,512]{3,2,1,0:T(8,128)(2,1)S(1)}, bf16[1,1,2048,512]{3,2,1,0:T(8,128)(2,1)}, u32[]{:S(2)}) copy-start(bf16[1,1,2048,512]{3,2,1,0:T(8,128)(2,1)} %param.17) | copy-start | bytes 6291460
  7.2 9.3 %copy-start.1 = (bf16[128,2048]{1,0:T(8,128)(2,1)S(1)}, bf16[128,2048]{1,0:T(8,128)(2,1)}, u32[]{:S(2)}) copy-start(bf16[128,2048]{1,0:T(8,128)(2,1)} %param.12) | copy-start | bytes 1572868
  16.5 3.3 copy-start.2
  35.2 115.5 %all-to-all-start = ((bf16[256,2,4224]{2,1,0:T(2,128)(2,1)}), bf16[256,2,4224]{2,1,0:T(2,128)(2,1)}, u32[]{:S(2)}, u32[]{:S(2)}) async-start(bf16[256,2,4224]{2,1,0:T(2,128)(2,1)} %reshape.131), calls=%async_computation | async-start | bytes 8650752 | tf_op jit(solution)/shard_map/all_to_all | solution.py:69
  51.7 239.4 %reduce-scatter.5.cloned.1.call-start = ((), (), s32[]{:S(2)}) async-start(), calls=%async_computation.5 | async-start | bytes 4718592 | tf_op jit(solution)/shard_map/reduce_scatter | solution.py:100
  159.0 5.4 %copy-start.3 = (bf16[512,4224]{1,0:T(8,128)(2,1)S(1)}, bf16[512,4224]{1,0:T(8,128)(2,1)}, u32[]{:S(2)}) copy-start(bf16[512,4224]{1,0:T(8,128)(2,1)} %reshape.132) | copy-start | bytes 12976132
  171.3 177.9 %reduce-scatter.3.cloned.1.call-start = ((), (), s32[]{:S(2)}) async-start(), calls=%async_computation.4 | async-start | bytes 9437184 | tf_op jit(solution)/shard_map/reduce_scatter | solution.py:97
  187.5 4.0 %copy-start.4 = (bf16[1,1,2048,1024]{3,2,1,0:T(8,128)(2,1)S(1)}, bf16[1,1,2048,1024]{3,2,1,0:T(8,128)(2,1)}, u32[]{:S(2)}) copy-start(bf16[1,1,2048,1024]{3,2,1,0:T(8,128)(2,1)} %param.16) | copy-start | bytes 12582916
  187.5 4.0 %copy-start.5 = (bf16[512,512]{0,1:T(8,128)(2,1)S(1)}, bf16[512,512]{0,1:T(8,128)(2,1)}, u32[]{:S(2)}) copy-start(bf16[512,512]{0,1:T(8,128)(2,1)} %get-tuple-element.43) | copy-start | bytes 1572868
  199.7 73.6 %all-to-all-start.1 = ((bf16[256,2,2176]{2,1,0:T(2,128)(2,1)}), bf16[256,2,2176]{2,1,0:T(2,128)(2,1)}, u32[]{:S(2)}, u32[]{:S(2)}) async-start(bf16[256,2,2176]{2,1,0:T(2,128)(2,1)} %reshape.134), calls=%async_computation.1 | async-start | bytes 4456448 | tf_op jit(solution)/shard_map/all_to_all | solution.py:82
Sparse Core Ops, SparseCore 0:
  171.4 74.0 reduce-scatter.4
  248.6 100.4 reduce-scatter.2

commit v2 on v1

--- a/solution.py
+++ b/solution.py
@@ -40,7 +40,7 @@
 def shards(tokens_in, grad_out, replica_of, gate_weights, placement, w_in_rep, w_down_rep):
     tok_count, model_width = tokens_in.shape
     top_count = replica_of.shape[1]
-    group_count = lax.axis_size("grp")
+    group_count = lax.axis_size("zl") * lax.axis_size("core")
     lane_count = lax.axis_size("ep")
     device_count = group_count * lane_count
     capacity = max(2, 2 * tok_count * top_count // device_count)
@@ -66,7 +66,7 @@
     outgoing = jnp.concatenate([send_x, send_dy, gate_cols], axis=1).reshape(
         device_count, capacity, 2 * model_width + lane_pad
     )
-    arrived = lax.all_to_all(outgoing, ("grp", "ep"), 0, 0, tiled=True).reshape(
+    arrived = lax.all_to_all(outgoing, ("zl", "core", "ep"), 0, 0, tiled=True).reshape(
         device_count * capacity, 2 * model_width + lane_pad
     )
     rows_x = arrived[:, :model_width]
@@ -79,7 +79,7 @@
     returning = jnp.concatenate([row_grad, back_cols], axis=1).reshape(
         device_count, capacity, model_width + lane_pad
     )
-    came_back = lax.all_to_all(returning, ("grp", "ep"), 0, 0, tiled=True).reshape(
+    came_back = lax.all_to_all(returning, ("zl", "core", "ep"), 0, 0, tiled=True).reshape(
         device_count * capacity, model_width + lane_pad
     )[send_slot]
     grads_rows = came_back[:, :model_width]
@@ -87,42 +87,56 @@
         grads_rows.reshape(tok_count, top_count, model_width).astype(jnp.float32), axis=1
     ).astype(jnp.bfloat16)
     d_gates = came_back[:, model_width].reshape(tok_count, top_count)
-    group_index = lax.axis_index("grp")
+    core_count = lax.axis_size("core")
+    core_index = lax.axis_index("core")
+    group_index = lax.axis_index("zl") * core_count + core_index
     column_index = lax.axis_index("ep")
-    my_slot = placement[group_index, column_index]
-    slot_mask = (jnp.arange(KPC, dtype=jnp.int32) == my_slot).astype(jnp.float32)
-    stack_in = slot_mask[:, None, None] * part_in[None]
-    stack_down = slot_mask[:, None, None] * part_down[None]
-    summed_in, summed_down = (
-        lax.psum_scatter(
-            stack_in.astype(jnp.bfloat16), "grp", scatter_dimension=1, tiled=True
-        ).astype(jnp.float32),
-        lax.psum_scatter(
-            stack_down.astype(jnp.bfloat16), "grp", scatter_dimension=1, tiled=True
-        ).astype(jnp.float32),
-    )
-    return (d_tokens, d_gates, summed_in.astype(jnp.bfloat16), summed_down.astype(jnp.bfloat16))
+    partner_index = group_index - core_index + (core_count - 1 - core_index)
+    own_slot = placement[group_index, column_index]
+    partner_slot = placement[partner_index, column_index]
+    hidden_width = part_down.shape[1]
+    parts = jnp.concatenate([part_in, part_down], axis=1).astype(jnp.bfloat16)
+    parts = parts.reshape(-1, core_count, model_width // group_count, parts.shape[1])
+    own_rows = jnp.take(parts, core_index, axis=1)
+    send_rows = jnp.take(parts, core_count - 1 - core_index, axis=1)
+    got_rows = lax.ppermute(send_rows, "core", [(0, 1), (1, 0)])
+    slots = jnp.arange(KPC, dtype=jnp.int32)
+    own_mask = (slots == own_slot).astype(jnp.float32)[:, None, None, None]
+    got_mask = (slots == partner_slot).astype(jnp.float32)[:, None, None, None]
+    stacked = (
+        own_mask * own_rows[None].astype(jnp.float32) + got_mask * got_rows[None].astype(jnp.float32)
+    ).astype(jnp.bfloat16)
+    summed = lax.psum_scatter(stacked, "zl", scatter_dimension=1, tiled=True)
+    summed = summed.reshape(KPC, model_width // group_count, -1)
+    width_in = summed.shape[2] - hidden_width
+    return (d_tokens, d_gates, summed[:, :, :width_in], summed[:, :, width_in:])
 
 
 def solution(mesh):
+    grp_size = mesh.shape["grp"]
+    core_size = 2
+    split_mesh = jax.sharding.Mesh(
+        mesh.devices.reshape(grp_size // core_size, core_size, mesh.shape["ep"]), ("zl", "core", "ep")
+    )
+    rows = ("zl", "core", "ep")
     placed = (
-        P(("grp", "ep"), None),
-        P(("grp", "ep"), None),
-        P(("grp", "ep"), None),
-        P(("grp", "ep"), None),
+        P(rows, None),
+        P(rows, None),
+        P(rows, None),
+        P(rows, None),
         P(),
-        P("grp", "ep", None, None),
-        P("grp", "ep", None, None),
+        P(("zl", "core"), "ep", None, None),
+        P(("zl", "core"), "ep", None, None),
     )
     return jax.shard_map(
         shards,
-        mesh=mesh,
+        mesh=split_mesh,
         in_specs=placed,
         out_specs=(
-            P(("grp", "ep"), None),
-            P(("grp", "ep"), None),
-            P("ep", "grp", None),
-            P("ep", "grp", None),
+            P(rows, None),
+            P(rows, None),
+            P("ep", ("zl", "core"), None),
+            P("ep", ("zl", "core"), None),
         ),
         check_vma=False,
     )

time: 358 us -> 359 us (level)
  matrix products: 22.2 us -> 16.6 us
  local copies, waits for them, and re-layouts: 47.1 us -> 51.5 us
    reduce_scatter x2 -> x1, waiting for transfers between devices: 58 us -> 23.8 us  [shards(): summed = lax.psum_scatter(stacked, 'zl', scatter_dimension=1, tiled=True)]
    all_to_all x2, waiting for transfers between devices: 162 us -> 196 us  [the longest x1 98.7 us: shards(): lax.all_to_all(outgoing, ('zl', 'core', 'ep'), 0, 0, tiled=True)]
    dot_general x1, matrix products: 7.29 us -> 2.43 us  [expert_backward(): lax.dot_general(rows_x, both_grad, (((0,), (0,)), ((), ())), preferred_el...]
    slice x0 -> x2, local copies, waits for them, and re-layouts: none -> 4.13 us  [shards(): return (d_tokens, d_gates, summed[:, :, :width_in], summed[:, :, width_in:])]
    convert_element_type x3 -> x4, other arithmetic: 12.1 us -> 12.6 us  [the longest x1 4.33 us: shards(): own_rows[None].astype(jnp.float32)]
  transfers between devices with their start and end apart: 4 -> 4, of which waited for: 3 -> 4; matrix products, arithmetic and copies ran while one was open for 13% -> 9% of each run, Pallas kernels for 0% -> 0%
where the time goes in v2:
time: 359 us; the launch traced here: 358 us
  waiting for transfers between devices  223 us (62%)
  local copies, waits for them, and re-layouts  51.5 us (14%)
  other arithmetic  27.5 us (8%)
  starting transfers between devices  24.9 us (7%)
  matrix products  16.6 us (5%)
  between operations  14.4 us (4%)
    all_to_all x1, waiting for transfers between devices, shards(): lax.all_to_all(outgoing, ('zl', 'core', 'ep'), 0, 0, tiled=True)  98.7 us
    all_to_all x1, waiting for transfers between devices, shards(): lax.all_to_all(returning, ('zl', 'core', 'ep'), 0, 0, tiled=True)  97.2 us
    reduce_scatter x1, waiting for transfers between devices, shards(): summed = lax.psum_scatter(stacked, 'zl', scatter_dimension=1, tiled=True)  23.8 us
    all_to_all x1, starting transfers between devices, shards(): lax.all_to_all(outgoing, ('zl', 'core', 'ep'), 0, 0, tiled=True)  16.5 us
    all_to_all x1, starting transfers between devices, shards(): lax.all_to_all(returning, ('zl', 'core', 'ep'), 0, 0, tiled=True)  8.04 us
    reshape x1, local copies, waits for them, and re-layouts, shards(): jnp.concatenate([send_x, send_dy, gate_cols], axis=1)  7.36 us
    reshape x1, local copies, waits for them, and re-layouts, shards(): lax.all_to_all(outgoing, ('zl', 'core', 'ep'), 0, 0, tiled=True)  7.29 us
  transfers between devices with their start and end apart: 4, of which 4 were waited for; matrix products, arithmetic and copies ran while one was open for 9% of the time, Pallas kernels for 0%

profile of v2, /device:TPU:1, one launch (start us, length us, event | category | flops | bytes accessed | tf_op | source)
XLA Modules:
  0.0 357.7 jit_solution(14686468816478697403)
XLA Ops:
  7.2 0.0 copy-start
  7.2 0.0 copy-start.1
  7.2 0.6 compare_reduce_fusion
  7.8 0.7 broadcast_multiply_fusion
  8.5 0.8 copy.23
  9.3 0.8 copy.24
  10.1 0.1 reshape.145
  10.3 0.1 copy.22
  10.4 0.1 mul.84
  10.5 0.1 eq.35
  10.7 0.2 convert_reduce_fusion.1
  10.9 1.4 scatter_custom_fusion
  12.3 3.4 gather_fusion.2
  15.7 0.7 select_select_fusion
  16.3 0.1 reshape.257
  16.5 0.0 copy-done.1
  16.5 0.0 copy-start.2
  16.5 3.3 gather_fusion.1
  19.8 0.0 copy-done.2
  19.8 3.3 gather_fusion
  23.1 2.6 broadcast_select_fusion.1
  25.7 2.2 fusion.2
  27.9 7.4 %reshape.147 = bf16[256,2,4224]{2,1,0:T(2,128)(2,1)} reshape(bf16[512,4224]{1,0:T(8,128)(2,1)} %fusion.2) | data formatting | bytes 8650752 | tf_op jit(solution)/shard_map/reshape | solution.py:66
  35.2 16.5 %all-to-all-start = ((bf16[256,2,4224]{2,1,0:T(2,128)(2,1)}), bf16[256,2,4224]{2,1,0:T(2,128)(2,1)}, u32[]{:S(2)}, u32[]{:S(2)}) async-start(bf16[256,2,4224]{2,1,0:T(2,128)(2,1)} %reshape.147), calls=%async_computation | async-start | bytes 8650752 | tf_op jit(solution)/shard_map/all_to_all | solution.py:69
  51.8 0.2 reduce-scatter.2.cloned.1.call-start
  52.0 98.7 %all-to-all-done = bf16[256,2,4224]{2,1,0:T(2,128)(2,1)} async-done(((bf16[256,2,4224]{2,1,0:T(2,128)(2,1)}), bf16[256,2,4224]{2,1,0:T(2,128)(2,1)}, u32[]{:S(2)}, u32[]{:S(2)}) %all-to-all-start) | async-done | bytes 4325408 | tf_op jit(solution)/shard_map/all_to_all | solution.py:69
  150.7 7.3 %reshape.148 = bf16[512,4224]{1,0:T(8,128)(2,1)} reshape(bf16[256,2,4224]{2,1,0:T(2,128)(2,1)} %all-to-all-done) | data formatting | bytes 8650752 | tf_op jit(solution)/shard_map/reshape | solution.py:69
  158.0 1.0 convert_reduce_fusion
  159.0 0.0 copy-start.4
  159.1 5.4 %fusion.7 = f32[512,1024]{0,1:T(8,128)S(1)} fusion(bf16[1,1,2048,1024]{3,2,1,0:T(8,128)(2,1)} %param.18, bf16[512,4224]{1,0:T(8,128)(2,1)} %reshape.148), kind=kOutput, calls=%fused_computation.21 | convolution fusion | flops 2147483648 | bytes 8388608 | tf_op jit(solution)/shard_map/dot_general | solution.py:11
  164.4 1.8 multiply_convert_fusion.2
  166.2 0.0 copy-start.6
  166.2 1.5 convolution_convert_fusion.1
  167.7 2.4 convolution_convert_fusion
  170.2 4.3 %fusion.15 = (f32[4,256,1536]{2,1,0:T(8,128)}, bf16[4,256,1536]{2,1,0:T(8,128)(2,1)}) fusion(s32[]{:T(128)S(6)} %select_n.64, bf16[4,2,256,1024]{3,2,1,0:T(8,128)(2,1)S(1)} %bitcast.30, bf16[4,2,256,512]{3,2,1,0:T(8,128)(2,1)S(1)} %bitcast.31, pred[]{:T(512)S(6)} %and.26, s32[]{:T(128)S(6)} %select_n.66, pred[]{:T(512)S(6)} %and.27), kind=kLoop, calls=%fused_computation.30 | loop fusion | flops 17301504 | bytes 15728650 | tf_op jit(solution)/shard_map/convert_element_type | solution.py:107
  174.5 0.1 collective-permute-start
  174.6 1.3 fusion.34
  176.0 1.3 compare_convert_fusion
  177.3 3.2 collective-permute-done
  180.5 2.7 convert_element_type.66
  183.3 0.0 copy-done.3
  183.3 4.3 %add_convert_fusion = bf16[2,4,256,1536]{3,2,0,1:T(8,128)(2,1)} fusion(f32[4,256,1536]{2,1,0:T(8,128)S(1)} %convert_element_type.66, f32[2]{0:T(128)S(1)} %get-tuple-element.67, f32[4,256,1536]{2,1,0:T(8,128)S(1)} %copy-done.3, f32[2]{0:T(128)S(1)} %get-tuple-element.68), kind=kLoop, calls=%fused_computation.5 | loop fusion | flops 12582912 | bytes 18874384 | tf_op jit(solution)/shard_map/convert_element_type | solution.py:108
  187.5 0.0 reduce-scatter.2.cloned.1.call-update
  187.6 0.0 copy-start.5
  187.6 0.0 copy-start.7
  187.6 3.1 fusion.4
  190.7 0.7 convert_select_fusion
  191.4 0.1 reshape.258
  191.5 2.4 fusion.16
  193.9 1.7 fusion.19
  195.6 4.3 %reshape.150 = bf16[256,2,2176]{2,1,0:T(2,128)(2,1)} reshape(bf16[512,2176]{1,0:T(8,128)(2,1)} %fusion.19) | data formatting | bytes 4456448 | tf_op jit(solution)/shard_map/reshape | solution.py:79
  199.9 8.0 %all-to-all-start.1 = ((bf16[256,2,2176]{2,1,0:T(2,128)(2,1)}), bf16[256,2,2176]{2,1,0:T(2,128)(2,1)}, u32[]{:S(2)}, u32[]{:S(2)}) async-start(bf16[256,2,2176]{2,1,0:T(2,128)(2,1)} %reshape.150), calls=%async_computation.1 | async-start | bytes 4456448 | tf_op jit(solution)/shard_map/all_to_all | solution.py:82
  208.0 97.2 %all-to-all-done.1 = bf16[256,2,2176]{2,1,0:T(2,128)(2,1)} async-done(((bf16[256,2,2176]{2,1,0:T(2,128)(2,1)}), bf16[256,2,2176]{2,1,0:T(2,128)(2,1)}, u32[]{:S(2)}, u32[]{:S(2)}) %all-to-all-start.1) | async-done | bytes 2228256 | tf_op jit(solution)/shard_map/all_to_all | solution.py:82
  305.2 4.2 %reshape.151 = bf16[512,2176]{1,0:T(8,128)(2,1)} reshape(bf16[256,2,2176]{2,1,0:T(2,128)(2,1)} %all-to-all-done.1) | data formatting | bytes 4456448 | tf_op jit(solution)/shard_map/reshape | solution.py:82
  309.4 4.5 %gather_fusion.3 = bf16[256,2176]{1,0:T(8,128)(2,1)S(1)} fusion(bf16[512,2176]{1,0:T(8,128)(2,1)} %reshape.151, s32[1024]{0:T(1024)S(1)} %pad_clamp_fusion), kind=kCustom, calls=%fused_computation.3 | custom fusion | bytes 2229248 | tf_op jit(solution)/shard_map/gather | solution.py:82
  313.9 1.1 slice.88
  315.0 2.5 reshape.152
  317.5 0.1 slice_reduce_fusion
  317.6 0.2 reshape_squeeze.3
  317.8 0.6 copy.29
  318.4 4.6 %reduce_sum.35 = bf16[128,2048]{1,0:T(8,128)(2,1)} reduce(bf16[128,2,2048]{2,1,0:T(2,128)(2,1)} %reshape.152, bf16[]{:T(256)} %constant.102.clone.1), dimensions={1}, to_apply=%region_4.5 | reduce | flops 262144 | bytes 1572866 | tf_op jit(solution)/shard_map/reduce_sum | solution.py:86
  323.0 23.8 %reduce-scatter.2.cloned.1.call-done = bf16[2,1,256,1536]{3,2,0,1:T(8,128)(2,1)} async-done(((bf16[2,4,256,1536]{3,2,0,1:T(8,128)(2,1)}), bf16[2,1,256,1536]{3,2,0,1:T(8,128)(2,1)}) %reduce-scatter.2.cloned.1.call-update) | async-done | bytes 1572880 | tf_op jit(solution)/shard_map/reduce_scatter | solution.py:109
  346.7 1.9 slice.91
  348.6 2.3 slice.90
  (11 shorter events, 0.0 us)
Async XLA Ops:
  7.2 157.2 %copy-start = (bf16[1,1,2048,512]{3,2,1,0:T(8,128)(2,1)S(1)}, bf16[1,1,2048,512]{3,2,1,0:T(8,128)(2,1)}, u32[]{:S(2)}) copy-start(bf16[1,1,2048,512]{3,2,1,0:T(8,128)(2,1)} %param.19) | copy-start | bytes 6291460
  7.2 9.3 %copy-start.1 = (bf16[128,2048]{1,0:T(8,128)(2,1)S(1)}, bf16[128,2048]{1,0:T(8,128)(2,1)}, u32[]{:S(2)}) copy-start(bf16[128,2048]{1,0:T(8,128)(2,1)} %param.14) | copy-start | bytes 1572868
  16.5 3.3 copy-start.2
  35.2 115.5 %all-to-all-start = ((bf16[256,2,4224]{2,1,0:T(2,128)(2,1)}), bf16[256,2,4224]{2,1,0:T(2,128)(2,1)}, u32[]{:S(2)}, u32[]{:S(2)}) async-start(bf16[256,2,4224]{2,1,0:T(2,128)(2,1)} %reshape.147), calls=%async_computation | async-start | bytes 8650752 | tf_op jit(solution)/shard_map/all_to_all | solution.py:69
  51.8 295.0 %reduce-scatter.2.cloned.1.call-start = ((), (), s32[]{:S(2)}) async-start(), calls=%async_computation.3 | async-start | bytes 7864320 | tf_op jit(solution)/shard_map/reduce_scatter | solution.py:109
  159.0 5.4 %copy-start.4 = (bf16[512,4224]{1,0:T(8,128)(2,1)S(1)}, bf16[512,4224]{1,0:T(8,128)(2,1)}, u32[]{:S(2)}) copy-start(bf16[512,4224]{1,0:T(8,128)(2,1)} %reshape.148) | copy-start | bytes 12976132
  166.2 1.5 copy-start.6
  174.5 6.0 %collective-permute-start = (bf16[4,256,1536]{2,1,0:T(8,128)(2,1)}, bf16[4,256,1536]{2,1,0:T(8,128)(2,1)}, u32[]{:S(2)}, u32[]{:S(2)}) collective-permute-start(bf16[4,256,1536]{2,1,0:T(8,128)(2,1)} %get-tuple-element.55), channel_id=1, source_target_pairs={{0,32},{32,0},{1,33},{33,1},{2,34},{34,2},{3,35},{35,3},{4,36},{36... | collective-permute-start | bytes 9437192 | tf_op jit(solution)/shard_map/ppermute | solution.py:102
  177.3 6.0 %copy-start.3 = (f32[4,256,1536]{2,1,0:T(8,128)S(1)}, f32[4,256,1536]{2,1,0:T(8,128)}, u32[]{:S(2)}) copy-start(f32[4,256,1536]{2,1,0:T(8,128)} %get-tuple-element.54) | copy-start | bytes 18874372
  187.6 4.0 %copy-start.5 = (bf16[1,1,2048,1024]{3,2,1,0:T(8,128)(2,1)S(1)}, bf16[1,1,2048,1024]{3,2,1,0:T(8,128)(2,1)}, u32[]{:S(2)}) copy-start(bf16[1,1,2048,1024]{3,2,1,0:T(8,128)(2,1)} %param.18) | copy-start | bytes 12582916
  187.6 3.9 %copy-start.7 = (bf16[512,512]{0,1:T(8,128)(2,1)S(1)}, bf16[512,512]{0,1:T(8,128)(2,1)}, u32[]{:S(2)}) copy-start(bf16[512,512]{0,1:T(8,128)(2,1)} %copy-done.6) | copy-start | bytes 1572868
  199.9 105.2 %all-to-all-start.1 = ((bf16[256,2,2176]{2,1,0:T(2,128)(2,1)}), bf16[256,2,2176]{2,1,0:T(2,128)(2,1)}, u32[]{:S(2)}, u32[]{:S(2)}) async-start(bf16[256,2,2176]{2,1,0:T(2,128)(2,1)} %reshape.150), calls=%async_computation.1 | async-start | bytes 4456448 | tf_op jit(solution)/shard_map/all_to_all | solution.py:82
Sparse Core Ops, SparseCore 0:
  187.7 159.0 reduce-scatter.1

commit v3 on v2

--- a/solution.py
+++ b/solution.py
@@ -49,9 +49,30 @@
     dest_rows = replica_of.reshape(-1)
     row_count = tok_count * top_count
     row_ids = jnp.arange(row_count, dtype=jnp.int32)
-    earlier = (dest_rows[:, None] == dest_rows[None, :]) & (row_ids[None, :] < row_ids[:, None])
+    core_count = lax.axis_size("core")
+    line_count = group_count // core_count
+    ring_count = 2 * line_count
+    my_group = lax.axis_index("zl") * core_count + lax.axis_index("core")
+    my_column = lax.axis_index("ep")
+    groups = jnp.arange(group_count, dtype=jnp.int32)
+    columns = jnp.arange(lane_count, dtype=jnp.int32)
+    z_of = (columns[None, :] // (lane_count // 2)) * line_count + (groups[:, None] // core_count)
+    my_z = (my_column // (lane_count // 2)) * line_count + my_group // core_count
+    hops = jnp.abs(z_of - my_z) % ring_count
+    hops = jnp.minimum(hops, ring_count - hops)
+    key = hops * (2 * group_count) + (groups[:, None] != my_group) * group_count + groups[:, None]
+    dest_group = dest_rows // lane_count
+    dest_column = dest_rows % lane_count
+    dest_expert = placement[dest_group, dest_column]
+    is_copy = placement[:, dest_column].T == dest_expert[:, None]
+    row_key = jnp.where(is_copy, key[:, dest_column].T, jnp.int32(1 << 20))
+    place = jnp.sum((row_key[:, None, :] < row_key[:, :, None]).astype(jnp.int32), axis=2)
+    expert_id = dest_column * KPC + dest_expert
+    earlier = (expert_id[:, None] == expert_id[None, :]) & (row_ids[None, :] < row_ids[:, None])
     rank_in = jnp.sum(earlier.astype(jnp.int32), axis=1)
-    send_slot = dest_rows * capacity + rank_in
+    pick = is_copy & (place == (rank_in // capacity)[:, None])
+    new_group = jnp.sum(jnp.where(pick, groups[None, :], 0), axis=1)
+    send_slot = (new_group * lane_count + dest_column) * capacity + rank_in % capacity
     slot_table = jnp.full((device_count * capacity,), -1, jnp.int32).at[send_slot].set(row_ids)
     is_live = slot_table >= 0
     safe_ids = jnp.maximum(slot_table, 0)

time: 359 us -> 363 us (1.011)
  local copies, waits for them, and re-layouts: 51.5 us -> 56 us
    gather x0 -> x5, local copies, waits for them, and re-layouts: none -> 3.79 us  [the longest x1 2.2 us: shards(): dest_expert = placement[dest_group, dest_column]]
where the time goes in v3:
time: 363 us; the launch traced here: 362 us
  waiting for transfers between devices  223 us (61%)
  local copies, waits for them, and re-layouts  56 us (15%)
  other arithmetic  27 us (7%)
  starting transfers between devices  24.9 us (7%)
  matrix products  16.6 us (5%)
  between operations  14.4 us (4%)
    all_to_all x1, waiting for transfers between devices, shards(): lax.all_to_all(outgoing, ('zl', 'core', 'ep'), 0, 0, tiled=True)  98.7 us
    all_to_all x1, waiting for transfers between devices, shards(): lax.all_to_all(returning, ('zl', 'core', 'ep'), 0, 0, tiled=True)  97.2 us
    reduce_scatter x1, waiting for transfers between devices, shards(): summed = lax.psum_scatter(stacked, 'zl', scatter_dimension=1, tiled=True)  23.8 us
    all_to_all x1, starting transfers between devices, shards(): lax.all_to_all(outgoing, ('zl', 'core', 'ep'), 0, 0, tiled=True)  16.5 us
    all_to_all x1, starting transfers between devices, shards(): lax.all_to_all(returning, ('zl', 'core', 'ep'), 0, 0, tiled=True)  8.03 us
    reshape x1, local copies, waits for them, and re-layouts, shards(): jnp.concatenate([send_x, send_dy, gate_cols], axis=1)  7.35 us
    reshape x1, local copies, waits for them, and re-layouts, shards(): lax.all_to_all(outgoing, ('zl', 'core', 'ep'), 0, 0, tiled=True)  7.3 us
  transfers between devices with their start and end apart: 4, of which 4 were waited for; matrix products, arithmetic and copies ran while one was open for 9% of the time, Pallas kernels for 0%

profile of v3, /device:TPU:1, one launch (start us, length us, event | category | flops | bytes accessed | tf_op | source)
XLA Modules:
  0.0 361.7 jit_solution(11906186316347487944)
XLA Ops:
  7.2 0.0 copy-start
  7.2 0.6 compare_reduce_fusion
  7.8 0.8 copy.37
  8.7 0.1 reshape.453
  8.8 0.1 reshape.452
  9.0 0.8 copy.38
  9.7 0.8 copy.42
  10.5 0.1 reshape.454
  10.7 2.2 gather_fusion.1
  12.9 0.2 convert_reduce_fusion.1
  13.1 0.1 fusion.32
  13.2 0.7 gather_fusion.2
  14.0 0.1 copy.40
  14.0 0.7 gather_fusion
  14.8 0.1 copy.39
  14.9 1.4 scatter_custom_fusion
  16.4 3.4 gather_fusion.5
  19.7 0.7 select_select_fusion
  20.4 0.1 reshape.588
  20.5 0.0 copy-start.2
  20.6 3.3 gather_fusion.4
  23.9 3.3 gather_fusion.3
  27.2 2.6 broadcast_select_fusion.1
  29.8 2.2 fusion.2
  31.9 7.3 %reshape.456 = bf16[256,2,4224]{2,1,0:T(2,128)(2,1)} reshape(bf16[512,4224]{1,0:T(8,128)(2,1)} %fusion.2) | data formatting | bytes 8650752 | tf_op jit(solution)/shard_map/reshape | solution.py:87
  39.3 16.5 %all-to-all-start = ((bf16[256,2,4224]{2,1,0:T(2,128)(2,1)}), bf16[256,2,4224]{2,1,0:T(2,128)(2,1)}, u32[]{:S(2)}, u32[]{:S(2)}) async-start(bf16[256,2,4224]{2,1,0:T(2,128)(2,1)} %reshape.456), calls=%async_computation | async-start | bytes 8650752 | tf_op jit(solution)/shard_map/all_to_all | solution.py:90
  55.8 0.2 reduce-scatter.2.cloned.1.call-start
  56.0 98.7 %all-to-all-done = bf16[256,2,4224]{2,1,0:T(2,128)(2,1)} async-done(((bf16[256,2,4224]{2,1,0:T(2,128)(2,1)}), bf16[256,2,4224]{2,1,0:T(2,128)(2,1)}, u32[]{:S(2)}, u32[]{:S(2)}) %all-to-all-start) | async-done | bytes 4325408 | tf_op jit(solution)/shard_map/all_to_all | solution.py:90
  154.8 7.3 %reshape.457 = bf16[512,4224]{1,0:T(8,128)(2,1)} reshape(bf16[256,2,4224]{2,1,0:T(2,128)(2,1)} %all-to-all-done) | data formatting | bytes 8650752 | tf_op jit(solution)/shard_map/reshape | solution.py:90
  162.1 1.0 convert_reduce_fusion
  163.1 5.3 %fusion.7 = f32[512,1024]{0,1:T(8,128)S(1)} fusion(bf16[1,1,2048,1024]{3,2,1,0:T(8,128)(2,1)} %param.18, bf16[512,4224]{1,0:T(8,128)(2,1)} %reshape.457), kind=kOutput, calls=%fused_computation.24 | convolution fusion | flops 2147483648 | bytes 8388608 | tf_op jit(solution)/shard_map/dot_general | solution.py:11
  168.5 1.8 multiply_convert_fusion.2
  170.3 0.0 copy-start.6
  170.3 1.5 convolution_convert_fusion.1
  171.8 2.4 convolution_convert_fusion
  174.2 4.3 %fusion.15 = (f32[4,256,1536]{2,1,0:T(8,128)}, bf16[4,256,1536]{2,1,0:T(8,128)(2,1)}) fusion(s32[]{:T(128)S(6)} %select_n.197, bf16[4,2,256,1024]{3,2,1,0:T(8,128)(2,1)S(1)} %bitcast.34, bf16[4,2,256,512]{3,2,1,0:T(8,128)(2,1)S(1)} %bitcast.35, pred[]{:T(512)S(6)} %and.174, s32[]{:T(128)S(6)} %select_n.199, pred[]{:T(512)S(6)} %and.175), kind=kLoop, calls=%fused_computation.33 | loop fusion | flops 17301504 | bytes 15728650 | tf_op jit(solution)/shard_map/convert_element_type | solution.py:128
  178.6 0.1 collective-permute-start
  178.7 1.3 fusion.47
  180.1 1.3 compare_convert_fusion
  181.4 3.2 collective-permute-done
  184.6 2.7 convert_element_type.71
  187.3 4.2 %add_convert_fusion = bf16[2,4,256,1536]{3,2,0,1:T(8,128)(2,1)} fusion(f32[4,256,1536]{2,1,0:T(8,128)S(1)} %convert_element_type.71, f32[2]{0:T(128)S(1)} %get-tuple-element.76, f32[4,256,1536]{2,1,0:T(8,128)S(1)} %copy-done.3, f32[2]{0:T(128)S(1)} %get-tuple-element.77), kind=kLoop, calls=%fused_computation.8 | loop fusion | flops 12582912 | bytes 18874384 | tf_op jit(solution)/shard_map/convert_element_type | solution.py:129
  191.6 0.0 reduce-scatter.2.cloned.1.call-update
  191.6 0.0 copy-start.5
  191.6 0.0 copy-start.7
  191.6 3.1 fusion.4
  194.7 0.7 convert_select_fusion
  195.4 0.1 reshape.589
  195.6 2.4 fusion.16
  198.0 1.7 fusion.19
  199.6 4.3 %reshape.459 = bf16[256,2,2176]{2,1,0:T(2,128)(2,1)} reshape(bf16[512,2176]{1,0:T(8,128)(2,1)} %fusion.19) | data formatting | bytes 4456448 | tf_op jit(solution)/shard_map/reshape | solution.py:100
  204.0 8.0 %all-to-all-start.1 = ((bf16[256,2,2176]{2,1,0:T(2,128)(2,1)}), bf16[256,2,2176]{2,1,0:T(2,128)(2,1)}, u32[]{:S(2)}, u32[]{:S(2)}) async-start(bf16[256,2,2176]{2,1,0:T(2,128)(2,1)} %reshape.459), calls=%async_computation.1 | async-start | bytes 4456448 | tf_op jit(solution)/shard_map/all_to_all | solution.py:103
  212.0 97.2 %all-to-all-done.1 = bf16[256,2,2176]{2,1,0:T(2,128)(2,1)} async-done(((bf16[256,2,2176]{2,1,0:T(2,128)(2,1)}), bf16[256,2,2176]{2,1,0:T(2,128)(2,1)}, u32[]{:S(2)}, u32[]{:S(2)}) %all-to-all-start.1) | async-done | bytes 2228256 | tf_op jit(solution)/shard_map/all_to_all | solution.py:103
  309.2 4.2 %reshape.460 = bf16[512,2176]{1,0:T(8,128)(2,1)} reshape(bf16[256,2,2176]{2,1,0:T(2,128)(2,1)} %all-to-all-done.1) | data formatting | bytes 4456448 | tf_op jit(solution)/shard_map/reshape | solution.py:103
  313.4 4.5 %gather_fusion.6 = bf16[256,2176]{1,0:T(8,128)(2,1)S(1)} fusion(bf16[512,2176]{1,0:T(8,128)(2,1)} %reshape.460, s32[1024]{0:T(1024)S(1)} %pad_clamp_fusion), kind=kCustom, calls=%fused_computation.6 | custom fusion | bytes 2229248 | tf_op jit(solution)/shard_map/gather | solution.py:103
  317.9 1.1 slice.94
  319.0 2.6 reshape.461
  321.6 0.1 slice_reduce_fusion
  321.7 0.2 reshape_squeeze.3
  321.8 0.6 copy.47
  322.4 4.6 %reduce_sum.55 = bf16[128,2048]{1,0:T(8,128)(2,1)} reduce(bf16[128,2,2048]{2,1,0:T(2,128)(2,1)} %reshape.461, bf16[]{:T(256)} %constant.214.clone.1), dimensions={1}, to_apply=%region_6.7 | reduce | flops 262144 | bytes 1572866 | tf_op jit(solution)/shard_map/reduce_sum | solution.py:107
  327.0 23.8 %reduce-scatter.2.cloned.1.call-done = bf16[2,1,256,1536]{3,2,0,1:T(8,128)(2,1)} async-done(((bf16[2,4,256,1536]{3,2,0,1:T(8,128)(2,1)}), bf16[2,1,256,1536]{3,2,0,1:T(8,128)(2,1)}) %reduce-scatter.2.cloned.1.call-update) | async-done | bytes 1572880 | tf_op jit(solution)/shard_map/reduce_scatter | solution.py:130
  350.8 1.9 slice.97
  352.6 2.3 slice.96
  (27 shorter events, 0.2 us)
Async XLA Ops:
  7.2 161.3 %copy-start = (bf16[1,1,2048,512]{3,2,1,0:T(8,128)(2,1)S(1)}, bf16[1,1,2048,512]{3,2,1,0:T(8,128)(2,1)}, u32[]{:S(2)}) copy-start(bf16[1,1,2048,512]{3,2,1,0:T(8,128)(2,1)} %param.19) | copy-start | bytes 6291460
  7.2 13.4 %copy-start.1 = (bf16[128,2048]{1,0:T(8,128)(2,1)S(1)}, bf16[128,2048]{1,0:T(8,128)(2,1)}, u32[]{:S(2)}) copy-start(bf16[128,2048]{1,0:T(8,128)(2,1)} %param.14) | copy-start | bytes 1572868
  20.5 3.3 copy-start.2
  39.3 115.5 %all-to-all-start = ((bf16[256,2,4224]{2,1,0:T(2,128)(2,1)}), bf16[256,2,4224]{2,1,0:T(2,128)(2,1)}, u32[]{:S(2)}, u32[]{:S(2)}) async-start(bf16[256,2,4224]{2,1,0:T(2,128)(2,1)} %reshape.456), calls=%async_computation | async-start | bytes 8650752 | tf_op jit(solution)/shard_map/all_to_all | solution.py:90
  55.8 294.9 %reduce-scatter.2.cloned.1.call-start = ((), (), s32[]{:S(2)}) async-start(), calls=%async_computation.3 | async-start | bytes 7864320 | tf_op jit(solution)/shard_map/reduce_scatter | solution.py:130
  163.1 5.4 %copy-start.4 = (bf16[512,4224]{1,0:T(8,128)(2,1)S(1)}, bf16[512,4224]{1,0:T(8,128)(2,1)}, u32[]{:S(2)}) copy-start(bf16[512,4224]{1,0:T(8,128)(2,1)} %reshape.457) | copy-start | bytes 12976132
  170.3 1.5 copy-start.6
  178.6 6.0 %collective-permute-start = (bf16[4,256,1536]{2,1,0:T(8,128)(2,1)}, bf16[4,256,1536]{2,1,0:T(8,128)(2,1)}, u32[]{:S(2)}, u32[]{:S(2)}) collective-permute-start(bf16[4,256,1536]{2,1,0:T(8,128)(2,1)} %get-tuple-element.64), channel_id=1, source_target_pairs={{0,32},{32,0},{1,33},{33,1},{2,34},{34,2},{3,35},{35,3},{4,36},{36... | collective-permute-start | bytes 9437192 | tf_op jit(solution)/shard_map/ppermute | solution.py:123
  181.4 6.0 %copy-start.3 = (f32[4,256,1536]{2,1,0:T(8,128)S(1)}, f32[4,256,1536]{2,1,0:T(8,128)}, u32[]{:S(2)}) copy-start(f32[4,256,1536]{2,1,0:T(8,128)} %get-tuple-element.63) | copy-start | bytes 18874372
  191.6 4.0 %copy-start.5 = (bf16[1,1,2048,1024]{3,2,1,0:T(8,128)(2,1)S(1)}, bf16[1,1,2048,1024]{3,2,1,0:T(8,128)(2,1)}, u32[]{:S(2)}) copy-start(bf16[1,1,2048,1024]{3,2,1,0:T(8,128)(2,1)} %param.18) | copy-start | bytes 12582916
  191.6 3.9 %copy-start.7 = (bf16[512,512]{0,1:T(8,128)(2,1)S(1)}, bf16[512,512]{0,1:T(8,128)(2,1)}, u32[]{:S(2)}) copy-start(bf16[512,512]{0,1:T(8,128)(2,1)} %copy-done.6) | copy-start | bytes 1572868
  204.0 105.2 %all-to-all-start.1 = ((bf16[256,2,2176]{2,1,0:T(2,128)(2,1)}), bf16[256,2,2176]{2,1,0:T(2,128)(2,1)}, u32[]{:S(2)}, u32[]{:S(2)}) async-start(bf16[256,2,2176]{2,1,0:T(2,128)(2,1)} %reshape.459), calls=%async_computation.1 | async-start | bytes 4456448 | tf_op jit(solution)/shard_map/all_to_all | solution.py:103
Sparse Core Ops, SparseCore 0:
  191.7 159.0 reduce-scatter.1

commit v4 on v2

--- a/solution.py
+++ b/solution.py
@@ -55,9 +55,12 @@
     slot_table = jnp.full((device_count * capacity,), -1, jnp.int32).at[send_slot].set(row_ids)
     is_live = slot_table >= 0
     safe_ids = jnp.maximum(slot_table, 0)
-    token_ids = safe_ids // top_count
-    send_x = jnp.where(is_live[:, None], tokens_in[token_ids], jnp.zeros((), tokens_in.dtype))
-    send_dy = jnp.where(is_live[:, None], grad_out[token_ids], jnp.zeros((), grad_out.dtype))
+    slot_token = jnp.where(is_live, safe_ids // top_count, -1)
+    pick_token = (slot_token[:, None] == jnp.arange(tok_count, dtype=jnp.int32)[None, :]).astype(
+        tokens_in.dtype
+    )
+    send_x = jnp.dot(pick_token, tokens_in, preferred_element_type=tokens_in.dtype)
+    send_dy = jnp.dot(pick_token, grad_out, preferred_element_type=grad_out.dtype)
     send_gate = jnp.where(
         is_live, gate_weights.reshape(-1)[safe_ids], jnp.zeros((), gate_weights.dtype)
     )
@@ -81,12 +84,16 @@
     )
     came_back = lax.all_to_all(returning, ("zl", "core", "ep"), 0, 0, tiled=True).reshape(
         device_count * capacity, model_width + lane_pad
-    )[send_slot]
-    grads_rows = came_back[:, :model_width]
-    d_tokens = jnp.sum(
-        grads_rows.reshape(tok_count, top_count, model_width).astype(jnp.float32), axis=1
+    )
+    slot_of_token = send_slot.reshape(tok_count, top_count)
+    slot_ids = jnp.arange(device_count * capacity, dtype=jnp.int32)
+    pick_slot = jnp.any(slot_of_token[:, :, None] == slot_ids[None, None, :], axis=1).astype(
+        came_back.dtype
+    )
+    d_tokens = jnp.dot(
+        pick_slot, came_back[:, :model_width], preferred_element_type=jnp.float32
     ).astype(jnp.bfloat16)
-    d_gates = came_back[:, model_width].reshape(tok_count, top_count)
+    d_gates = came_back[:, model_width][send_slot].reshape(tok_count, top_count)
     core_count = lax.axis_size("core")
     core_index = lax.axis_index("core")
     group_index = lax.axis_index("zl") * core_count + core_index

time: 359 us -> 351 us (0.978)
  local copies, waits for them, and re-layouts: 51.5 us -> 39.7 us
  other arithmetic: 27.5 us -> 19.8 us
  waiting for transfers between devices: 223 us -> 230 us
  matrix products: 16.6 us -> 22 us
    gather x3 -> x1, local copies, waits for them, and re-layouts: 11.1 us -> 1.93 us  [shards(): d_gates = came_back[:, model_width][send_slot].reshape(tok_count, top_count)]
    reduce_scatter x1, waiting for transfers between devices: 23.8 us -> 30.8 us  [shards(): summed = lax.psum_scatter(stacked, 'zl', scatter_dimension=1, tiled=True)]
    dot_general x0 -> x3, matrix products: none -> 5.37 us  [the longest x1 2.83 us: shards(): jnp.dot(pick_slot, came_back[:, :model_width], preferred_element_type=jnp...]
    reduce_sum x1 -> x0, other arithmetic: 4.57 us -> none  [shards(): jnp.sum(grads_rows.reshape(tok_count, top_count, model_width).astype(jnp....]
  transfers between devices with their start and end apart: 4 -> 4, of which waited for: 4 -> 4; matrix products, arithmetic and copies ran while one was open for 9% -> 7% of each run, Pallas kernels for 0% -> 0%
where the time goes in v4:
time: 351 us; the launch traced here: 350 us
  waiting for transfers between devices  230 us (66%)
  local copies, waits for them, and re-layouts  39.7 us (11%)
  starting transfers between devices  24.9 us (7%)
  matrix products  22 us (6%)
  other arithmetic  19.8 us (6%)
  between operations  14.4 us (4%)
    all_to_all x1, waiting for transfers between devices, shards(): lax.all_to_all(outgoing, ('zl', 'core', 'ep'), 0, 0, tiled=True)  98.7 us
    all_to_all x1, waiting for transfers between devices, shards(): lax.all_to_all(returning, ('zl', 'core', 'ep'), 0, 0, tiled=True)  97 us
    reduce_scatter x1, waiting for transfers between devices, shards(): summed = lax.psum_scatter(stacked, 'zl', scatter_dimension=1, tiled=True)  30.8 us
    all_to_all x1, starting transfers between devices, shards(): lax.all_to_all(outgoing, ('zl', 'core', 'ep'), 0, 0, tiled=True)  16.5 us
    all_to_all x1, starting transfers between devices, shards(): lax.all_to_all(returning, ('zl', 'core', 'ep'), 0, 0, tiled=True)  8.01 us
    reshape x1, local copies, waits for them, and re-layouts, shards(): jnp.concatenate([send_x, send_dy, gate_cols], axis=1)  7.35 us
    reshape x1, local copies, waits for them, and re-layouts, shards(): lax.all_to_all(outgoing, ('zl', 'core', 'ep'), 0, 0, tiled=True)  7.3 us
  transfers between devices with their start and end apart: 4, of which 4 were waited for; matrix products, arithmetic and copies ran while one was open for 7% of the time, Pallas kernels for 0%

profile of v4, /device:TPU:1, one launch (start us, length us, event | category | flops | bytes accessed | tf_op | source)
XLA Modules:
  0.0 350.4 jit_solution(1849832914011548197)
XLA Ops:
  7.2 0.0 copy-start
  7.2 0.0 copy-start.3
  7.2 0.6 compare_reduce_fusion
  7.8 0.8 copy.34
  8.6 0.1 reshape.151
  8.8 0.8 copy.31
  9.6 0.1 eq.61
  9.7 0.2 convert_reduce_fusion.1
  9.9 0.1 reduce_sum.23
  10.1 0.1 mul.86
  10.2 1.4 scatter_custom_fusion
  11.7 3.4 gather_fusion
  15.1 0.7 select_select_fusion
  15.7 0.1 reshape.245
  15.8 1.8 fusion.30
  17.6 0.0 copy-done.3
  17.7 0.8 fusion.31
  18.4 2.2 fusion.2
  20.6 7.3 %reshape.153 = bf16[256,2,4224]{2,1,0:T(2,128)(2,1)} reshape(bf16[512,4224]{1,0:T(8,128)(2,1)} %fusion.2) | data formatting | bytes 8650752 | tf_op jit(solution)/shard_map/reshape | solution.py:69
  27.9 16.5 %all-to-all-start = ((bf16[256,2,4224]{2,1,0:T(2,128)(2,1)}), bf16[256,2,4224]{2,1,0:T(2,128)(2,1)}, u32[]{:S(2)}, u32[]{:S(2)}) async-start(bf16[256,2,4224]{2,1,0:T(2,128)(2,1)} %reshape.153), calls=%async_computation | async-start | bytes 8650752 | tf_op jit(solution)/shard_map/all_to_all | solution.py:72
  44.5 0.2 reduce-scatter.2.cloned.1.call-start
  44.7 98.7 %all-to-all-done = bf16[256,2,4224]{2,1,0:T(2,128)(2,1)} async-done(((bf16[256,2,4224]{2,1,0:T(2,128)(2,1)}), bf16[256,2,4224]{2,1,0:T(2,128)(2,1)}, u32[]{:S(2)}, u32[]{:S(2)}) %all-to-all-start) | async-done | bytes 4325408 | tf_op jit(solution)/shard_map/all_to_all | solution.py:72
  143.4 7.3 %reshape.154 = bf16[512,4224]{1,0:T(8,128)(2,1)} reshape(bf16[256,2,4224]{2,1,0:T(2,128)(2,1)} %all-to-all-done) | data formatting | bytes 8650752 | tf_op jit(solution)/shard_map/reshape | solution.py:72
  150.7 1.0 convert_reduce_fusion
  151.8 0.0 copy-start.2
  151.8 5.4 %fusion.7 = f32[512,1024]{0,1:T(8,128)S(1)} fusion(bf16[1,1,2048,1024]{3,2,1,0:T(8,128)(2,1)} %param.18, bf16[512,4224]{1,0:T(8,128)(2,1)} %reshape.154), kind=kOutput, calls=%fused_computation.19 | convolution fusion | flops 2147483648 | bytes 8388608 | tf_op jit(solution)/shard_map/dot_general | solution.py:11
  157.1 0.0 copy-done
  157.1 0.0 copy-done.2
  157.1 1.8 multiply_convert_fusion.2
  159.0 0.0 copy-start.5
  159.0 1.5 convolution_convert_fusion.1
  160.5 0.0 copy-done.5
  160.5 2.4 convolution_convert_fusion
  162.9 4.3 %fusion.15 = (f32[4,256,1536]{2,1,0:T(8,128)}, bf16[4,256,1536]{2,1,0:T(8,128)(2,1)}) fusion(s32[]{:T(128)S(6)} %select_n.55, bf16[4,2,256,1024]{3,2,1,0:T(8,128)(2,1)S(1)} %bitcast.33, bf16[4,2,256,512]{3,2,1,0:T(8,128)(2,1)S(1)} %bitcast.34, pred[]{:T(512)S(6)} %and.26, s32[]{:T(128)S(6)} %select_n.57, pred[]{:T(512)S(6)} %and.27), kind=kLoop, calls=%fused_computation.28 | loop fusion | flops 17301504 | bytes 15728650 | tf_op jit(solution)/shard_map/convert_element_type | solution.py:114
  167.3 0.1 collective-permute-start
  167.4 1.3 fusion.42
  168.7 1.3 compare_convert_fusion
  170.0 3.2 collective-permute-done
  173.3 2.7 convert_element_type.70
  176.0 4.2 %add_convert_fusion = bf16[2,4,256,1536]{3,2,0,1:T(8,128)(2,1)} fusion(f32[4,256,1536]{2,1,0:T(8,128)S(1)} %convert_element_type.70, f32[2]{0:T(128)S(1)} %get-tuple-element.64, f32[4,256,1536]{2,1,0:T(8,128)S(1)} %copy-done.1, f32[2]{0:T(128)S(1)} %get-tuple-element.65), kind=kLoop, calls=%fused_computation.3 | loop fusion | flops 12582912 | bytes 18874384 | tf_op jit(solution)/shard_map/convert_element_type | solution.py:115
  180.2 0.0 reduce-scatter.2.cloned.1.call-update
  180.3 0.0 copy-start.4
  180.3 0.0 copy-start.6
  180.3 3.2 fusion.4
  183.4 0.7 convert_select_fusion
  184.1 0.1 reshape.246
  184.2 0.0 copy-done.4
  184.2 0.0 copy-done.6
  184.3 2.4 fusion.16
  186.6 1.7 fusion.19
  188.3 4.3 %reshape.156 = bf16[256,2,2176]{2,1,0:T(2,128)(2,1)} reshape(bf16[512,2176]{1,0:T(8,128)(2,1)} %fusion.19) | data formatting | bytes 4456448 | tf_op jit(solution)/shard_map/reshape | solution.py:82
  192.7 8.0 %all-to-all-start.1 = ((bf16[256,2,2176]{2,1,0:T(2,128)(2,1)}), bf16[256,2,2176]{2,1,0:T(2,128)(2,1)}, u32[]{:S(2)}, u32[]{:S(2)}) async-start(bf16[256,2,2176]{2,1,0:T(2,128)(2,1)} %reshape.156), calls=%async_computation.1 | async-start | bytes 4456448 | tf_op jit(solution)/shard_map/all_to_all | solution.py:85
  200.7 0.1 copy.33
  200.7 0.1 fusion.29
  200.9 97.0 %all-to-all-done.1 = bf16[256,2,2176]{2,1,0:T(2,128)(2,1)} async-done(((bf16[256,2,2176]{2,1,0:T(2,128)(2,1)}), bf16[256,2,2176]{2,1,0:T(2,128)(2,1)}, u32[]{:S(2)}, u32[]{:S(2)}) %all-to-all-start.1) | async-done | bytes 2228256 | tf_op jit(solution)/shard_map/all_to_all | solution.py:85
  297.9 4.2 %reshape.157 = bf16[512,2176]{1,0:T(8,128)(2,1)} reshape(bf16[256,2,2176]{2,1,0:T(2,128)(2,1)} %all-to-all-done.1) | data formatting | bytes 4456448 | tf_op jit(solution)/shard_map/reshape | solution.py:85
  302.1 1.0 slice_reduce_fusion
  303.1 1.9 gather_fusion.1
  305.1 0.2 reshape.158
  305.2 0.6 copy.39
  305.8 2.8 convolution_convert_fusion.2
  308.7 30.8 %reduce-scatter.2.cloned.1.call-done = bf16[2,1,256,1536]{3,2,0,1:T(8,128)(2,1)} async-done(((bf16[2,4,256,1536]{3,2,0,1:T(8,128)(2,1)}), bf16[2,1,256,1536]{3,2,0,1:T(8,128)(2,1)}) %reduce-scatter.2.cloned.1.call-update) | async-done | bytes 1572880 | tf_op jit(solution)/shard_map/reduce_scatter | solution.py:116
  339.4 1.9 slice.87
  341.3 2.3 slice.86
  (8 shorter events, 0.0 us)
Async XLA Ops:
  7.2 150.0 %copy-start = (bf16[1,1,2048,512]{3,2,1,0:T(8,128)(2,1)S(1)}, bf16[1,1,2048,512]{3,2,1,0:T(8,128)(2,1)}, u32[]{:S(2)}) copy-start(bf16[1,1,2048,512]{3,2,1,0:T(8,128)(2,1)} %param.19) | copy-start | bytes 6291460
  7.2 10.5 %copy-start.3 = (bf16[128,2048]{1,0:T(8,128)(2,1)S(1)}, bf16[128,2048]{1,0:T(8,128)(2,1)}, u32[]{:S(2)}) copy-start(bf16[128,2048]{1,0:T(8,128)(2,1)} %param.13) | copy-start | bytes 1572868
  27.9 115.5 %all-to-all-start = ((bf16[256,2,4224]{2,1,0:T(2,128)(2,1)}), bf16[256,2,4224]{2,1,0:T(2,128)(2,1)}, u32[]{:S(2)}, u32[]{:S(2)}) async-start(bf16[256,2,4224]{2,1,0:T(2,128)(2,1)} %reshape.153), calls=%async_computation | async-start | bytes 8650752 | tf_op jit(solution)/shard_map/all_to_all | solution.py:72
  44.5 295.0 %reduce-scatter.2.cloned.1.call-start = ((), (), s32[]{:S(2)}) async-start(), calls=%async_computation.3 | async-start | bytes 7864320 | tf_op jit(solution)/shard_map/reduce_scatter | solution.py:116
  151.8 5.4 %copy-start.2 = (bf16[512,4224]{1,0:T(8,128)(2,1)S(1)}, bf16[512,4224]{1,0:T(8,128)(2,1)}, u32[]{:S(2)}) copy-start(bf16[512,4224]{1,0:T(8,128)(2,1)} %reshape.154) | copy-start | bytes 12976132
  159.0 1.5 copy-start.5
  167.3 6.0 %collective-permute-start = (bf16[4,256,1536]{2,1,0:T(8,128)(2,1)}, bf16[4,256,1536]{2,1,0:T(8,128)(2,1)}, u32[]{:S(2)}, u32[]{:S(2)}) collective-permute-start(bf16[4,256,1536]{2,1,0:T(8,128)(2,1)} %get-tuple-element.55), channel_id=1, source_target_pairs={{0,32},{32,0},{1,33},{33,1},{2,34},{34,2},{3,35},{35,3},{4,36},{36... | collective-permute-start | bytes 9437192 | tf_op jit(solution)/shard_map/ppermute | solution.py:109
  170.0 6.0 %copy-start.1 = (f32[4,256,1536]{2,1,0:T(8,128)S(1)}, f32[4,256,1536]{2,1,0:T(8,128)}, u32[]{:S(2)}) copy-start(f32[4,256,1536]{2,1,0:T(8,128)} %get-tuple-element.54) | copy-start | bytes 18874372
  180.3 4.0 %copy-start.4 = (bf16[1,1,2048,1024]{3,2,1,0:T(8,128)(2,1)S(1)}, bf16[1,1,2048,1024]{3,2,1,0:T(8,128)(2,1)}, u32[]{:S(2)}) copy-start(bf16[1,1,2048,1024]{3,2,1,0:T(8,128)(2,1)} %param.18) | copy-start | bytes 12582916
  180.3 4.0 %copy-start.6 = (bf16[512,512]{0,1:T(8,128)(2,1)S(1)}, bf16[512,512]{0,1:T(8,128)(2,1)}, u32[]{:S(2)}) copy-start(bf16[512,512]{0,1:T(8,128)(2,1)} %copy-done.5) | copy-start | bytes 1572868
  192.7 105.2 %all-to-all-start.1 = ((bf16[256,2,2176]{2,1,0:T(2,128)(2,1)}), bf16[256,2,2176]{2,1,0:T(2,128)(2,1)}, u32[]{:S(2)}, u32[]{:S(2)}) async-start(bf16[256,2,2176]{2,1,0:T(2,128)(2,1)} %reshape.156), calls=%async_computation.1 | async-start | bytes 4456448 | tf_op jit(solution)/shard_map/all_to_all | solution.py:85
Sparse Core Ops, SparseCore 0:
  180.4 159.0 reduce-scatter.1

commit v5 on v4

--- a/solution.py
+++ b/solution.py
@@ -101,23 +101,27 @@
     partner_index = group_index - core_index + (core_count - 1 - core_index)
     own_slot = placement[group_index, column_index]
     partner_slot = placement[partner_index, column_index]
-    hidden_width = part_down.shape[1]
-    parts = jnp.concatenate([part_in, part_down], axis=1).astype(jnp.bfloat16)
-    parts = parts.reshape(-1, core_count, model_width // group_count, parts.shape[1])
-    own_rows = jnp.take(parts, core_index, axis=1)
-    send_rows = jnp.take(parts, core_count - 1 - core_index, axis=1)
-    got_rows = lax.ppermute(send_rows, "core", [(0, 1), (1, 0)])
     slots = jnp.arange(KPC, dtype=jnp.int32)
     own_mask = (slots == own_slot).astype(jnp.float32)[:, None, None, None]
     got_mask = (slots == partner_slot).astype(jnp.float32)[:, None, None, None]
-    stacked = (
-        own_mask * own_rows[None].astype(jnp.float32) + got_mask * got_rows[None].astype(jnp.float32)
-    ).astype(jnp.bfloat16)
-    summed = lax.psum_scatter(stacked, "zl", scatter_dimension=1, tiled=True)
-    summed = summed.reshape(KPC, model_width // group_count, -1)
-    width_in = summed.shape[2] - hidden_width
-    return (d_tokens, d_gates, summed[:, :, :width_in], summed[:, :, width_in:])
 
+    def reduce_copies(part):
+        part = part.astype(jnp.bfloat16).reshape(
+            -1, core_count, model_width // group_count, part.shape[1]
+        )
+        own_rows = jnp.take(part, core_index, axis=1)
+        send_rows = jnp.take(part, core_count - 1 - core_index, axis=1)
+        got_rows = lax.ppermute(send_rows, "core", [(0, 1), (1, 0)])
+        stacked = (
+            own_mask * own_rows[None].astype(jnp.float32)
+            + got_mask * got_rows[None].astype(jnp.float32)
+        ).astype(jnp.bfloat16)
+        summed = lax.psum_scatter(stacked, "zl", scatter_dimension=1, tiled=True)
+        return summed.reshape(KPC, model_width // group_count, -1)
+
+    summed_down = reduce_copies(part_down)
+    summed_in = reduce_copies(part_in)
+    return (d_tokens, d_gates, summed_in, summed_down)
 
 def solution(mesh):
     grp_size = mesh.shape["grp"]

time: 351 us -> 337 us (0.960)
  waiting for transfers between devices: 230 us -> 218 us
    all_to_all x1, waiting for transfers between devices: 97 us -> 62.7 us  [shards(): lax.all_to_all(returning, ('zl', 'core', 'ep'), 0, 0, tiled=True)]
    reduce_scatter x1 -> x2, waiting for transfers between devices: 30.8 us -> 52.2 us  [reduce_copies(): summed = lax.psum_scatter(stacked, 'zl', scatter_dimension=1, tiled=True)]
    slice x2 -> x0, local copies, waits for them, and re-layouts: 4.13 us -> none  [shards(): return (d_tokens, d_gates, summed[:, :, :width_in], summed[:, :, width_in:])]
    convert_element_type x3 -> x6, other arithmetic: 11.3 us -> 8.66 us  [the longest x2 4.76 us: reduce_copies(): stacked = (own_mask * own_rows[None].astype(jnp.float32) + got_mask * got...]
  transfers between devices with their start and end apart: 4 -> 6, of which waited for: 4 -> 4; matrix products, arithmetic and copies ran while one was open for 7% -> 10% of each run, Pallas kernels for 0% -> 0%
where the time goes in v5:
time: 337 us; the launch traced here: 336 us
  waiting for transfers between devices  218 us (65%)
  local copies, waits for them, and re-layouts  36.6 us (11%)
  starting transfers between devices  25.4 us (8%)
  matrix products  24.5 us (7%)
  other arithmetic  17 us (5%)
  between operations  14.4 us (4%)
    all_to_all x1, waiting for transfers between devices, shards(): lax.all_to_all(outgoing, ('zl', 'core', 'ep'), 0, 0, tiled=True)  98.9 us
    all_to_all x1, waiting for transfers between devices, shards(): lax.all_to_all(returning, ('zl', 'core', 'ep'), 0, 0, tiled=True)  62.7 us
    reduce_scatter x2, waiting for transfers between devices, reduce_copies(): summed = lax.psum_scatter(stacked, 'zl', scatter_dimension=1, tiled=True)  52.2 us
    all_to_all x1, starting transfers between devices, shards(): lax.all_to_all(outgoing, ('zl', 'core', 'ep'), 0, 0, tiled=True)  16.5 us
    all_to_all x1, starting transfers between devices, shards(): lax.all_to_all(returning, ('zl', 'core', 'ep'), 0, 0, tiled=True)  8.24 us
    reshape x1, local copies, waits for them, and re-layouts, shards(): jnp.concatenate([send_x, send_dy, gate_cols], axis=1)  7.35 us
    reshape x1, local copies, waits for them, and re-layouts, shards(): lax.all_to_all(outgoing, ('zl', 'core', 'ep'), 0, 0, tiled=True)  7.3 us
  transfers between devices with their start and end apart: 6, of which 4 were waited for; matrix products, arithmetic and copies ran while one was open for 10% of the time, Pallas kernels for 0%

profile of v5, /device:TPU:1, one launch (start us, length us, event | category | flops | bytes accessed | tf_op | source)
XLA Modules:
  0.0 335.6 jit_solution(9813959998264657318)
XLA Ops:
  7.2 0.0 copy-start
  7.2 0.0 copy-start.3
  7.2 0.6 compare_reduce_fusion
  7.8 0.8 copy.34
  8.6 0.1 reshape.160
  8.8 0.8 copy.31
  9.6 0.1 eq.61
  9.7 0.2 convert_reduce_fusion.1
  9.9 0.1 reduce_sum.23
  10.1 0.1 mul.112
  10.2 1.4 scatter_custom_fusion
  11.7 3.4 %gather_fusion = bf16[512]{0:T(512)(128)(2,1)S(1)} fusion(bf16[256]{0:T(256)(128)(2,1)S(1)} %reshape.160, s32[1024]{0:T(1024)S(1)} %pad_clamp_fusion.1), kind=kCustom, calls=%fused_computation | custom fusion | bytes 4096 | tf_op jit(solution)/shard_map/gather | solution.py:65
  15.1 0.7 select_select_fusion
  15.7 0.1 reshape.316
  15.8 1.8 fusion.23
  17.7 0.8 fusion.24
  18.4 2.2 fusion.2
  20.6 7.4 %reshape.162 = bf16[256,2,4224]{2,1,0:T(2,128)(2,1)} reshape(bf16[512,4224]{1,0:T(8,128)(2,1)} %fusion.2) | data formatting | bytes 8650752 | tf_op jit(solution)/shard_map/reshape | solution.py:69
  28.0 16.5 %all-to-all-start = ((bf16[256,2,4224]{2,1,0:T(2,128)(2,1)}), bf16[256,2,4224]{2,1,0:T(2,128)(2,1)}, u32[]{:S(2)}, u32[]{:S(2)}) async-start(bf16[256,2,4224]{2,1,0:T(2,128)(2,1)} %reshape.162), calls=%async_computation | async-start | bytes 8650752 | tf_op jit(solution)/shard_map/all_to_all | solution.py:72
  44.5 0.0 reduce-scatter.5.cloned.1.call-start
  44.5 98.9 %all-to-all-done = bf16[256,2,4224]{2,1,0:T(2,128)(2,1)} async-done(((bf16[256,2,4224]{2,1,0:T(2,128)(2,1)}), bf16[256,2,4224]{2,1,0:T(2,128)(2,1)}, u32[]{:S(2)}, u32[]{:S(2)}) %all-to-all-start) | async-done | bytes 4325408 | tf_op jit(solution)/shard_map/all_to_all | solution.py:72
  143.5 7.3 %reshape.163 = bf16[512,4224]{1,0:T(8,128)(2,1)} reshape(bf16[256,2,4224]{2,1,0:T(2,128)(2,1)} %all-to-all-done) | data formatting | bytes 8650752 | tf_op jit(solution)/shard_map/reshape | solution.py:72
  150.8 1.0 convert_reduce_fusion
  151.8 5.3 %fusion.7 = f32[512,1024]{0,1:T(8,128)S(1)} fusion(bf16[1,1,2048,1024]{3,2,1,0:T(8,128)(2,1)} %param.20, bf16[512,4224]{1,0:T(8,128)(2,1)} %reshape.163), kind=kOutput, calls=%fused_computation.15 | convolution fusion | flops 2147483648 | bytes 8388608 | tf_op jit(solution)/shard_map/dot_general | solution.py:11
  157.2 2.8 multiply_convert_fusion.2
  160.0 1.5 convolution_convert_fusion.1
  161.4 0.0 copy-done.5
  161.5 1.5 bitcast_convert_fusion.1
  163.0 0.1 collective-permute-start.1
  163.1 1.4 fusion.35
  164.6 1.3 compare_convert_fusion
  165.9 0.0 collective-permute-done.1
  165.9 1.5 convert_element_type.90
  167.4 0.0 copy-start.7
  167.4 2.0 add_convert_fusion.1
  169.5 0.0 reduce-scatter.5.cloned.1.call-update
  169.5 0.0 reduce-scatter.3.cloned.1.call-start
  169.5 0.0 copy-done.7
  169.5 0.0 copy-done.8
  169.6 4.0 %convolution_convert_fusion = bf16[2048,1024]{1,0:T(8,128)(2,1)S(1)} fusion(bf16[512,4224]{1,0:T(8,128)(2,1)} %reshape.163, bf16[512,512]{0,1:T(8,128)(2,1)S(1)} %copy-done.8, bf16[512,512]{0,1:T(8,128)(2,1)S(1)} %copy-done.7), kind=kOutput, calls=%fused_computation.18 | convolution fusion | flops 2151677952 | bytes 7340032 | tf_op jit(solution)/shard_map/dot_general | solution.py:31
  173.6 0.4 bitcast_convert_fusion
  174.0 0.5 collective-permute-start
  174.4 3.8 %collective-permute-done = bf16[4,256,1024]{2,1,0:T(8,128)(2,1)S(1)} collective-permute-done((bf16[4,256,1024]{2,1,0:T(8,128)(2,1)S(1)}, bf16[4,256,1024]{2,1,0:T(8,128)(2,1)S(1)}, u32[]{:S(2)}, u32[]{:S(2)}) %collective-permute-start) | collective-permute-done | bytes 2097184 | tf_op jit(solution)/shard_map/ppermute | solution.py:114
  178.2 0.4 convert_element_type.86
  178.7 2.7 add_convert_fusion
  181.4 0.0 reduce-scatter.3.cloned.1.call-update
  181.4 1.0 copy-done.6
  182.5 3.1 fusion.4
  185.6 0.7 convert_select_fusion
  186.3 0.1 reshape.317
  186.4 2.4 fusion.9
  188.8 1.6 fusion.12
  190.4 4.2 %reshape.165 = bf16[256,2,2176]{2,1,0:T(2,128)(2,1)} reshape(bf16[512,2176]{1,0:T(8,128)(2,1)} %fusion.12) | data formatting | bytes 4456448 | tf_op jit(solution)/shard_map/reshape | solution.py:82
  194.6 8.2 %all-to-all-start.1 = ((bf16[256,2,2176]{2,1,0:T(2,128)(2,1)}), bf16[256,2,2176]{2,1,0:T(2,128)(2,1)}, u32[]{:S(2)}, u32[]{:S(2)}) async-start(bf16[256,2,2176]{2,1,0:T(2,128)(2,1)} %reshape.165), calls=%async_computation.1 | async-start | bytes 4456448 | tf_op jit(solution)/shard_map/all_to_all | solution.py:85
  202.9 0.1 copy.33
  203.0 0.1 fusion.22
  203.1 62.7 %all-to-all-done.1 = bf16[256,2,2176]{2,1,0:T(2,128)(2,1)} async-done(((bf16[256,2,2176]{2,1,0:T(2,128)(2,1)}), bf16[256,2,2176]{2,1,0:T(2,128)(2,1)}, u32[]{:S(2)}, u32[]{:S(2)}) %all-to-all-start.1) | async-done | bytes 2228256 | tf_op jit(solution)/shard_map/all_to_all | solution.py:85
  265.8 4.2 %reshape.166 = bf16[512,2176]{1,0:T(8,128)(2,1)} reshape(bf16[256,2,2176]{2,1,0:T(2,128)(2,1)} %all-to-all-done.1) | data formatting | bytes 4456448 | tf_op jit(solution)/shard_map/reshape | solution.py:85
  270.0 1.0 slice_reduce_fusion
  271.0 1.9 gather_fusion.1
  272.9 0.2 reshape.167
  273.1 0.6 copy.39
  273.7 2.8 convolution_convert_fusion.2
  276.5 52.2 %reduce-scatter.3.cloned.1.call-done = bf16[2,1,256,1024]{3,2,0,1:T(8,128)(2,1)} async-done(((bf16[2,4,256,1024]{3,2,0,1:T(8,128)(2,1)}), bf16[2,1,256,1024]{3,2,0,1:T(8,128)(2,1)}) %reduce-scatter.3.cloned.1.call-update) | async-done | bytes 1048592 | tf_op jit(solution)/shard_map/reduce_scatter | solution.py:119
  (20 shorter events, 0.1 us)
Async XLA Ops:
  7.2 150.0 %copy-start = (bf16[1,1,2048,512]{3,2,1,0:T(8,128)(2,1)S(1)}, bf16[1,1,2048,512]{3,2,1,0:T(8,128)(2,1)}, u32[]{:S(2)}) copy-start(bf16[1,1,2048,512]{3,2,1,0:T(8,128)(2,1)} %param.21) | copy-start | bytes 6291460
  7.2 10.5 %copy-start.3 = (bf16[128,2048]{1,0:T(8,128)(2,1)S(1)}, bf16[128,2048]{1,0:T(8,128)(2,1)}, u32[]{:S(2)}) copy-start(bf16[128,2048]{1,0:T(8,128)(2,1)} %param.15) | copy-start | bytes 1572868
  28.0 115.5 %all-to-all-start = ((bf16[256,2,4224]{2,1,0:T(2,128)(2,1)}), bf16[256,2,4224]{2,1,0:T(2,128)(2,1)}, u32[]{:S(2)}, u32[]{:S(2)}) async-start(bf16[256,2,4224]{2,1,0:T(2,128)(2,1)} %reshape.162), calls=%async_computation | async-start | bytes 8650752 | tf_op jit(solution)/shard_map/all_to_all | solution.py:72
  44.5 232.0 %reduce-scatter.5.cloned.1.call-start = ((), (), s32[]{:S(2)}) async-start(), calls=%async_computation.5 | async-start | bytes 2621440 | tf_op jit(solution)/shard_map/reduce_scatter | solution.py:119
  151.8 5.4 %copy-start.2 = (bf16[512,4224]{1,0:T(8,128)(2,1)S(1)}, bf16[512,4224]{1,0:T(8,128)(2,1)}, u32[]{:S(2)}) copy-start(bf16[512,4224]{1,0:T(8,128)(2,1)} %reshape.163) | copy-start | bytes 12976132
  160.0 1.5 copy-start.5
  163.0 2.9 collective-permute-start.1
  163.1 4.3 %copy-start.1 = (f32[4,256,512]{2,1,0:T(8,128)S(1)}, f32[4,256,512]{2,1,0:T(8,128)}, u32[]{:S(2)}) copy-start(f32[4,256,512]{2,1,0:T(8,128)} %get-tuple-element.70) | copy-start | bytes 6291460
  167.4 2.1 copy-start.7
  167.4 2.1 copy-start.8
  169.5 159.2 %reduce-scatter.3.cloned.1.call-start = ((), (), s32[]{:S(2)}) async-start(), calls=%async_computation.4 | async-start | bytes 5242880 | tf_op jit(solution)/shard_map/reduce_scatter | solution.py:119
  174.0 4.2 %collective-permute-start = (bf16[4,256,1024]{2,1,0:T(8,128)(2,1)S(1)}, bf16[4,256,1024]{2,1,0:T(8,128)(2,1)S(1)}, u32[]{:S(2)}, u32[]{:S(2)}) collective-permute-start(bf16[4,256,1024]{2,1,0:T(8,128)(2,1)S(1)} %get-tuple-element.67), channel_id=1, source_target_pairs={{0,32},{32,0},{1,33},{33,1},{2,34},{34,2},{3,35},{35,3},{4,36},{36... | collective-permute-start | bytes 6291464 | tf_op jit(solution)/shard_map/ppermute | solution.py:114
  181.4 1.0 copy-start.6
  182.4 3.9 %copy-start.4 = (bf16[1,1,2048,1024]{3,2,1,0:T(8,128)(2,1)S(1)}, bf16[1,1,2048,1024]{3,2,1,0:T(8,128)(2,1)}, u32[]{:S(2)}) copy-start(bf16[1,1,2048,1024]{3,2,1,0:T(8,128)(2,1)} %param.20) | copy-start | bytes 12582916
  182.5 3.9 %copy-start.9 = (bf16[512,512]{0,1:T(8,128)(2,1)S(1)}, bf16[512,512]{0,1:T(8,128)(2,1)}, u32[]{:S(2)}) copy-start(bf16[512,512]{0,1:T(8,128)(2,1)} %get-tuple-element.69) | copy-start | bytes 1572868
  194.6 71.1 %all-to-all-start.1 = ((bf16[256,2,2176]{2,1,0:T(2,128)(2,1)}), bf16[256,2,2176]{2,1,0:T(2,128)(2,1)}, u32[]{:S(2)}, u32[]{:S(2)}) async-start(bf16[256,2,2176]{2,1,0:T(2,128)(2,1)} %reshape.165), calls=%async_computation.1 | async-start | bytes 4456448 | tf_op jit(solution)/shard_map/all_to_all | solution.py:85
Sparse Core Ops, SparseCore 0:
  169.6 66.3 reduce-scatter.4
  239.2 89.5 reduce-scatter.2

commit v6 on v5

--- a/solution.py
+++ b/solution.py
@@ -105,7 +105,7 @@
     own_mask = (slots == own_slot).astype(jnp.float32)[:, None, None, None]
     got_mask = (slots == partner_slot).astype(jnp.float32)[:, None, None, None]
 
-    def reduce_copies(part):
+    def reduce_copies(part, on_core):
         part = part.astype(jnp.bfloat16).reshape(
             -1, core_count, model_width // group_count, part.shape[1]
         )
@@ -116,11 +116,14 @@
             own_mask * own_rows[None].astype(jnp.float32)
             + got_mask * got_rows[None].astype(jnp.float32)
         ).astype(jnp.bfloat16)
+        if on_core:
+            gathered = lax.all_to_all(stacked, "zl", 1, 1, tiled=True)
+            return jnp.sum(gathered.astype(jnp.float32), axis=1).astype(jnp.bfloat16)
         summed = lax.psum_scatter(stacked, "zl", scatter_dimension=1, tiled=True)
         return summed.reshape(KPC, model_width // group_count, -1)
 
-    summed_down = reduce_copies(part_down)
-    summed_in = reduce_copies(part_in)
+    summed_down = reduce_copies(part_down, True)
+    summed_in = reduce_copies(part_in, False)
     return (d_tokens, d_gates, summed_in, summed_down)
 
 def solution(mesh):

time: 337 us -> 371 us (1.10)
  waiting for transfers between devices: 218 us -> 242 us
  other arithmetic: 17 us -> 24.3 us
  starting transfers between devices: 25.4 us -> 32.2 us
    all_to_all x0 -> x1, waiting for transfers between devices: none -> 91.5 us  [reduce_copies(): gathered = lax.all_to_all(stacked, 'zl', 1, 1, tiled=True)]
    reduce_scatter x2 -> x1, waiting for transfers between devices: 52.2 us -> 0.01 us  [reduce_copies(): summed = lax.psum_scatter(stacked, 'zl', scatter_dimension=1, tiled=True)]
    all_to_all x1, waiting for transfers between devices: 62.7 us -> 51.4 us  [shards(): lax.all_to_all(returning, ('zl', 'core', 'ep'), 0, 0, tiled=True)]
    all_to_all x0 -> x1, starting transfers between devices: none -> 4.73 us  [reduce_copies(): gathered = lax.all_to_all(stacked, 'zl', 1, 1, tiled=True)]
    ppermute x2, waiting for transfers between devices: 3.79 us -> 0.01 us  [reduce_copies(): got_rows = lax.ppermute(send_rows, 'core', [(0, 1), (1, 0)])]
  transfers between devices with their start and end apart: 6 -> 6, of which waited for: 4 -> 3; matrix products, arithmetic and copies ran while one was open for 10% -> 11% of each run, Pallas kernels for 0% -> 0%
where the time goes in v6:
time: 371 us; the launch traced here: 370 us
  waiting for transfers between devices  242 us (65%)
  local copies, waits for them, and re-layouts  35.6 us (10%)
  starting transfers between devices  32.2 us (9%)
  other arithmetic  24.3 us (7%)
  matrix products  22 us (6%)
  between operations  14.4 us (4%)
    all_to_all x1, waiting for transfers between devices, shards(): lax.all_to_all(outgoing, ('zl', 'core', 'ep'), 0, 0, tiled=True)  98.7 us
    all_to_all x1, waiting for transfers between devices, reduce_copies(): gathered = lax.all_to_all(stacked, 'zl', 1, 1, tiled=True)  91.5 us
    all_to_all x1, waiting for transfers between devices, shards(): lax.all_to_all(returning, ('zl', 'core', 'ep'), 0, 0, tiled=True)  51.4 us
    all_to_all x1, starting transfers between devices, shards(): lax.all_to_all(outgoing, ('zl', 'core', 'ep'), 0, 0, tiled=True)  16.5 us
    all_to_all x1, starting transfers between devices, shards(): lax.all_to_all(returning, ('zl', 'core', 'ep'), 0, 0, tiled=True)  10.2 us
  transfers between devices with their start and end apart: 6, of which 3 were waited for; matrix products, arithmetic and copies ran while one was open for 11% of the time, Pallas kernels for 0%

profile of v6, /device:TPU:1, one launch (start us, length us, event | category | flops | bytes accessed | tf_op | source)
XLA Modules:
  0.0 370.2 jit_solution(588617031691309564)
XLA Ops:
  7.2 0.0 copy-start
  7.2 0.6 compare_reduce_fusion
  7.8 0.8 copy.42
  8.6 0.1 reshape.157
  8.8 0.8 copy.39
  9.6 0.1 eq.61
  9.7 0.2 convert_reduce_fusion.1
  9.9 0.1 reduce_sum.35
  10.1 0.1 mul.112
  10.2 1.4 scatter_custom_fusion
  11.7 3.4 gather_fusion
  15.1 0.7 select_select_fusion
  15.7 0.1 reshape.312
  15.8 1.8 fusion.23
  17.7 0.8 fusion.24
  18.4 2.2 fusion.2
  20.6 7.3 %reshape.159 = bf16[256,2,4224]{2,1,0:T(2,128)(2,1)} reshape(bf16[512,4224]{1,0:T(8,128)(2,1)} %fusion.2) | data formatting | bytes 8650752 | tf_op jit(solution)/shard_map/reshape | solution.py:69
  27.9 16.5 %all-to-all-start = ((bf16[256,2,4224]{2,1,0:T(2,128)(2,1)}), bf16[256,2,4224]{2,1,0:T(2,128)(2,1)}, u32[]{:S(2)}, u32[]{:S(2)}) async-start(bf16[256,2,4224]{2,1,0:T(2,128)(2,1)} %reshape.159), calls=%async_computation | async-start | bytes 8650752 | tf_op jit(solution)/shard_map/all_to_all | solution.py:72
  44.4 0.2 reduce-scatter.2.cloned.1.call-start
  44.7 98.7 %all-to-all-done = bf16[256,2,4224]{2,1,0:T(2,128)(2,1)} async-done(((bf16[256,2,4224]{2,1,0:T(2,128)(2,1)}), bf16[256,2,4224]{2,1,0:T(2,128)(2,1)}, u32[]{:S(2)}, u32[]{:S(2)}) %all-to-all-start) | async-done | bytes 4325408 | tf_op jit(solution)/shard_map/all_to_all | solution.py:72
  143.4 7.3 %reshape.160 = bf16[512,4224]{1,0:T(8,128)(2,1)} reshape(bf16[256,2,4224]{2,1,0:T(2,128)(2,1)} %all-to-all-done) | data formatting | bytes 8650752 | tf_op jit(solution)/shard_map/reshape | solution.py:72
  150.7 1.0 convert_reduce_fusion
  151.7 5.3 %fusion.7 = f32[512,1024]{0,1:T(8,128)S(1)} fusion(bf16[1,1,2048,1024]{3,2,1,0:T(8,128)(2,1)} %param.20, bf16[512,4224]{1,0:T(8,128)(2,1)} %reshape.160), kind=kOutput, calls=%fused_computation.15 | convolution fusion | flops 2147483648 | bytes 8388608 | tf_op jit(solution)/shard_map/dot_general | solution.py:11
  157.1 1.8 multiply_convert_fusion.2
  158.9 0.0 copy-start.10
  158.9 0.0 copy-start.6
  158.9 2.4 convolution_convert_fusion
  161.4 0.0 copy-done.8
  161.4 0.0 copy-done.10
  161.4 3.1 bitcast_convert_fusion
  164.4 0.1 collective-permute-start
  164.6 1.5 convolution_convert_fusion.1
  166.1 1.6 bitcast_convert_fusion.1
  167.7 0.4 collective-permute-start.1
  168.0 1.4 fusion.35
  169.5 1.2 compare_convert_fusion
  170.7 0.0 collective-permute-done
  170.7 2.0 convert_element_type.88
  172.7 2.8 add_convert_fusion
  175.5 0.0 reduce-scatter.2.cloned.1.call-update
  175.5 0.0 collective-permute-done.1
  175.5 1.6 convert_element_type.92
  177.2 0.2 copy-done.2
  177.4 2.1 add_convert_fusion.1
  179.5 4.7 %all-to-all-start.2 = ((bf16[2,4,256,512]{3,2,0,1:T(8,128)(2,1)}), bf16[2,4,256,512]{3,2,0,1:T(8,128)(2,1)}, u32[]{:S(2)}, u32[]{:S(2)}) async-start(bf16[2,4,256,512]{3,2,0,1:T(8,128)(2,1)} %add_convert_fusion.1), calls=%async_computation.3 | async-start | bytes 4194304 | tf_op jit(solution)/shard_map/all_to_all | solution.py:120
  184.2 0.0 copy-start.11
  184.3 3.1 fusion.4
  187.4 0.7 convert_select_fusion
  188.0 0.1 reshape.313
  188.2 2.4 fusion.9
  190.6 1.6 fusion.12
  192.2 4.2 %reshape.162 = bf16[256,2,2176]{2,1,0:T(2,128)(2,1)} reshape(bf16[512,2176]{1,0:T(8,128)(2,1)} %fusion.12) | data formatting | bytes 4456448 | tf_op jit(solution)/shard_map/reshape | solution.py:82
  196.4 91.5 %all-to-all-done.2 = bf16[2,4,256,512]{3,2,0,1:T(8,128)(2,1)} async-done(((bf16[2,4,256,512]{3,2,0,1:T(8,128)(2,1)}), bf16[2,4,256,512]{3,2,0,1:T(8,128)(2,1)}, u32[]{:S(2)}, u32[]{:S(2)}) %all-to-all-start.2) | async-done | bytes 2097184 | tf_op jit(solution)/shard_map/all_to_all | solution.py:120
  287.9 10.2 %all-to-all-start.1 = ((bf16[256,2,2176]{2,1,0:T(2,128)(2,1)}), bf16[256,2,2176]{2,1,0:T(2,128)(2,1)}, u32[]{:S(2)}, u32[]{:S(2)}) async-start(bf16[256,2,2176]{2,1,0:T(2,128)(2,1)} %reshape.162), calls=%async_computation.1 | async-start | bytes 4456448 | tf_op jit(solution)/shard_map/all_to_all | solution.py:85
  298.1 0.1 copy.41
  298.2 0.1 fusion.22
  298.3 2.9 reduce_sum.38
  301.2 51.4 %all-to-all-done.1 = bf16[256,2,2176]{2,1,0:T(2,128)(2,1)} async-done(((bf16[256,2,2176]{2,1,0:T(2,128)(2,1)}), bf16[256,2,2176]{2,1,0:T(2,128)(2,1)}, u32[]{:S(2)}, u32[]{:S(2)}) %all-to-all-start.1) | async-done | bytes 2228256 | tf_op jit(solution)/shard_map/all_to_all | solution.py:85
  352.6 4.2 %reshape.163 = bf16[512,2176]{1,0:T(8,128)(2,1)} reshape(bf16[256,2,2176]{2,1,0:T(2,128)(2,1)} %all-to-all-done.1) | data formatting | bytes 4456448 | tf_op jit(solution)/shard_map/reshape | solution.py:85
  356.8 1.0 slice_reduce_fusion
  357.8 1.9 gather_fusion.1
  359.8 0.2 reshape.164
  359.9 0.6 copy.47
  360.5 2.8 convolution_convert_fusion.2
  (24 shorter events, 0.1 us)
Async XLA Ops:
  7.2 149.9 %copy-start = (bf16[1,1,2048,512]{3,2,1,0:T(8,128)(2,1)S(1)}, bf16[1,1,2048,512]{3,2,1,0:T(8,128)(2,1)}, u32[]{:S(2)}) copy-start(bf16[1,1,2048,512]{3,2,1,0:T(8,128)(2,1)} %param.21) | copy-start | bytes 6291460
  7.2 10.5 %copy-start.4 = (bf16[128,2048]{1,0:T(8,128)(2,1)S(1)}, bf16[128,2048]{1,0:T(8,128)(2,1)}, u32[]{:S(2)}) copy-start(bf16[128,2048]{1,0:T(8,128)(2,1)} %param.15) | copy-start | bytes 1572868
  27.9 115.5 %all-to-all-start = ((bf16[256,2,4224]{2,1,0:T(2,128)(2,1)}), bf16[256,2,4224]{2,1,0:T(2,128)(2,1)}, u32[]{:S(2)}, u32[]{:S(2)}) async-start(bf16[256,2,4224]{2,1,0:T(2,128)(2,1)} %reshape.159), calls=%async_computation | async-start | bytes 8650752 | tf_op jit(solution)/shard_map/all_to_all | solution.py:72
  44.4 318.9 %reduce-scatter.2.cloned.1.call-start = ((), (), s32[]{:S(2)}) async-start(), calls=%async_computation.4 | async-start | bytes 5242880 | tf_op jit(solution)/shard_map/reduce_scatter | solution.py:122
  151.7 5.4 %copy-start.3 = (bf16[512,4224]{1,0:T(8,128)(2,1)S(1)}, bf16[512,4224]{1,0:T(8,128)(2,1)}, u32[]{:S(2)}) copy-start(bf16[512,4224]{1,0:T(8,128)(2,1)} %reshape.160) | copy-start | bytes 12976132
  158.9 2.5 copy-start.8
  158.9 2.5 copy-start.10
  158.9 5.7 %copy-start.6 = (bf16[512,512]{0,1:T(8,128)(2,1)}, bf16[512,512]{0,1:T(8,128)(2,1)S(1)}, u32[]{:S(2)}) copy-start(bf16[512,512]{0,1:T(8,128)(2,1)S(1)} %get-tuple-element.76) | copy-start | bytes 1572868
  164.4 6.2 %collective-permute-start = (bf16[4,256,1024]{2,1,0:T(8,128)(2,1)}, bf16[4,256,1024]{2,1,0:T(8,128)(2,1)}, u32[]{:S(2)}, u32[]{:S(2)}) collective-permute-start(bf16[4,256,1024]{2,1,0:T(8,128)(2,1)} %get-tuple-element.71), channel_id=1, source_target_pairs={{0,32},{32,0},{1,33},{33,1},{2,34},{34,2},{3,35},{35,3},{4,36},{36... | collective-permute-start | bytes 6291464 | tf_op jit(solution)/shard_map/ppermute | solution.py:114
  167.7 7.9 %collective-permute-start.1 = (bf16[4,256,512]{2,1,0:T(8,128)(2,1)S(1)}, bf16[4,256,512]{2,1,0:T(8,128)(2,1)}, u32[]{:S(2)}, u32[]{:S(2)}) collective-permute-start(bf16[4,256,512]{2,1,0:T(8,128)(2,1)S(1)} %get-tuple-element.75), channel_id=1, source_target_pairs={{0,32},{32,0},{1,33},{33,1},{2,34},{34,2},{3,35},{35,3},{4,36},{36... | collective-permute-start | bytes 3145736 | tf_op jit(solution)/shard_map/ppermute | solution.py:114
  168.0 4.7 %copy-start.1 = (f32[4,256,1024]{2,1,0:T(8,128)S(1)}, f32[4,256,1024]{2,1,0:T(8,128)}, u32[]{:S(2)}) copy-start(f32[4,256,1024]{2,1,0:T(8,128)} %get-tuple-element.70) | copy-start | bytes 12582916
  175.5 1.9 copy-start.2
  177.4 6.8 %copy-start.7 = (bf16[512,512]{0,1:T(8,128)(2,1)S(1)}, bf16[512,512]{0,1:T(8,128)(2,1)}, u32[]{:S(2)}) copy-start(bf16[512,512]{0,1:T(8,128)(2,1)} %copy-done.6) | copy-start | bytes 1572868
  179.5 108.4 %all-to-all-start.2 = ((bf16[2,4,256,512]{3,2,0,1:T(8,128)(2,1)}), bf16[2,4,256,512]{3,2,0,1:T(8,128)(2,1)}, u32[]{:S(2)}, u32[]{:S(2)}) async-start(bf16[2,4,256,512]{3,2,0,1:T(8,128)(2,1)} %add_convert_fusion.1), calls=%async_computation.3 | async-start | bytes 4194304 | tf_op jit(solution)/shard_map/all_to_all | solution.py:120
  184.2 3.9 %copy-start.5 = (bf16[1,1,2048,1024]{3,2,1,0:T(8,128)(2,1)S(1)}, bf16[1,1,2048,1024]{3,2,1,0:T(8,128)(2,1)}, u32[]{:S(2)}) copy-start(bf16[1,1,2048,1024]{3,2,1,0:T(8,128)(2,1)} %param.20) | copy-start | bytes 12582916
  184.2 4.0 %copy-start.9 = (bf16[512,512]{0,1:T(8,128)(2,1)S(1)}, bf16[512,512]{0,1:T(8,128)(2,1)}, u32[]{:S(2)}) copy-start(bf16[512,512]{0,1:T(8,128)(2,1)} %copy-done.8) | copy-start | bytes 1572868
  184.2 4.0 %copy-start.11 = (bf16[512,512]{0,1:T(8,128)(2,1)S(1)}, bf16[512,512]{0,1:T(8,128)(2,1)}, u32[]{:S(2)}) copy-start(bf16[512,512]{0,1:T(8,128)(2,1)} %copy-done.10) | copy-start | bytes 1572868
  287.9 64.7 %all-to-all-start.1 = ((bf16[256,2,2176]{2,1,0:T(2,128)(2,1)}), bf16[256,2,2176]{2,1,0:T(2,128)(2,1)}, u32[]{:S(2)}, u32[]{:S(2)}) async-start(bf16[256,2,2176]{2,1,0:T(2,128)(2,1)} %reshape.162), calls=%async_computation.1 | async-start | bytes 4456448 | tf_op jit(solution)/shard_map/all_to_all | solution.py:85
Sparse Core Ops, SparseCore 0:
  175.6 113.6 reduce-scatter.1
